TPU v7x, 512 devices: a whole 4x8x8 slice. The times are simulated.
512 devices in a mesh: dp: 16 (over x_lo, y), space: 32 (over x_hi, z, core).
Axes of the slice: x: 4 (x_hi: 2, x_lo: 2; x = x_hi * 2 + x_lo), y: 8, z: 8, core: 2. Of those that a mesh axis runs over, the one named last changes fastest.
Arguments:
- inputs: bfloat16 [16, 10, 64, 32, 128], P('dp', None, 'space'), may hold values from -8 to 8
- land_mask: int32 [16, 10, 64, 32], P('dp', None, 'space'), may hold values 0 or 1
- weight_one: float32 [128, 27, 128], P('dp'), may hold values from -0.109375 to 0.109375
- weight_two: float32 [128, 27, 128], P('dp'), may hold values from -0.109375 to 0.109375
- cotangent: bfloat16 [16, 10, 64, 32, 128], P('dp', None, 'space'), may hold values from -6 to 6
Outputs:
- prediction: bfloat16 [16, 10, 64, 32, 128], P('dp', None, 'space')
- input_grad: bfloat16 [16, 10, 64, 32, 128], P('dp', None, 'space')
- grad_one: float32 [128, 27, 128], P('dp')
- grad_two: float32 [128, 27, 128], P('dp')
All inputs are finite; a program needn't handle non-finite values. No bound on the sum of `land_mask` on one device may be relied on, other than what follows from the above.
Results may differ from a plain program's by a relative error of at most 0.0067.
Values may be sent and summed in bfloat16 or wider, within the bound.
No kernel may reach another device: no remote copies, remote signals or barrier semaphores. Data moves between devices by JAX's collectives and lax.ppermute only.
A program may use at most 64 MiB of HBM per device.

v0:
```python
import jax
import jax.numpy as jnp
from jax import lax
from jax.sharding import PartitionSpec as P


def with_halo(cells, sides, width):
    for axis, dim in sides:
        count = lax.axis_size(axis)
        ends = count - 1
        head = lax.slice_in_dim(cells, 0, width, axis=dim)
        tail = lax.slice_in_dim(cells, cells.shape[dim] - width, cells.shape[dim], axis=dim)
        cells = jnp.concatenate(
            [
                lax.ppermute(tail, axis, [(i, (i + 1) % count) for i in range(ends)]),
                cells,
                lax.ppermute(head, axis, [((i + 1) % count, i) for i in range(ends)]),
            ],
            axis=dim,
        )
    return cells


def widen(field):
    rimmed = with_halo(field, (("space", 2),), 1)
    return jnp.pad(rimmed, ((0, 0), (1, 1), (0, 0), (1, 1), (0, 0)))


def group_window(padded, depth_off, mirrored, shape):
    depth, rows, columns = shape
    pieces = []
    for row_off in range(3):
        for col_off in range(3):
            row_at = 2 - row_off if mirrored else row_off
            col_at = 2 - col_off if mirrored else col_off
            piece = padded[
                :,
                depth_off : depth_off + depth,
                row_at : row_at + rows,
                col_at : col_at + columns,
                :,
            ]
            pieces.append(piece.reshape(-1, padded.shape[4]))
    return jnp.concatenate(pieces, axis=1)


def conv_full(padded, kernel, shape):
    channel = kernel.shape[0]
    total = None
    for group in range(3):
        window = group_window(padded, group, False, shape)
        block = jnp.transpose(kernel[:, 9 * group : 9 * group + 9, :], (1, 0, 2)).reshape(
            9 * channel, kernel.shape[2]
        )
        term = jnp.dot(window, block, preferred_element_type=jnp.float32)
        total = term if total is None else total + term
    return total


def transpose_part(padded, kernel, shape):
    channel = kernel.shape[0]
    total = None
    for group in range(3):
        window = group_window(padded, 2 - group, True, shape)
        block = kernel[:, 9 * group : 9 * group + 9, :].reshape(channel, 9 * kernel.shape[2])
        term = lax.dot_general(
            window, block, (((1,), (1,)), ((), ())), preferred_element_type=jnp.float32
        )
        total = term if total is None else total + term
    return total


def local_grad(padded, back_flat, shape):
    channel = padded.shape[4]
    terms = []
    for group in range(3):
        window = group_window(padded, group, False, shape)
        block = lax.dot_general(
            window, back_flat, (((0,), (0,)), ((), ())), preferred_element_type=jnp.float32
        )
        terms.append(jnp.transpose(block.reshape(9, channel, back_flat.shape[1]), (1, 0, 2)))
    return jnp.concatenate(terms, axis=1)


def kernel_again(kernel):
    return lax.all_gather(kernel, "dp", axis=0, tiled=True)


def reduce_grad(grad_full):
    owned = lax.psum_scatter(grad_full, "dp", scatter_dimension=0, tiled=True)
    return lax.psum(owned, "space")


def on_device(inputs, land_mask, weight_one, weight_two, cotangent):
    samples, depth, rows, columns, channel = inputs.shape
    shape = (depth, rows, columns)
    kernel_one = weight_one.astype(jnp.bfloat16)
    kernel_two = weight_two.astype(jnp.bfloat16)
    scale = land_mask.reshape(-1, 1).astype(jnp.float32)
    in_pad = widen(inputs)
    pre_one = conv_full(in_pad, kernel_again(kernel_one), shape)
    act_one = (scale * jax.nn.silu(pre_one)).astype(jnp.bfloat16).reshape(inputs.shape)
    act_pad = widen(act_one)
    pre_two = conv_full(act_pad, kernel_again(kernel_two), shape)
    prediction = (scale * pre_two).astype(jnp.bfloat16).reshape(inputs.shape)
    back_two = (cotangent.reshape(-1, channel).astype(jnp.float32) * scale).astype(jnp.bfloat16)
    back_pad = widen(back_two.reshape(inputs.shape))
    grad_two = reduce_grad(local_grad(act_pad, back_two, shape))
    pull_one = transpose_part(back_pad, kernel_again(kernel_two), shape)
    sigma = jax.nn.sigmoid(pre_one)
    back_one = (pull_one * scale * sigma * (1.0 + pre_one * (1.0 - sigma))).astype(jnp.bfloat16)
    first_pad = widen(back_one.reshape(inputs.shape))
    grad_one = reduce_grad(local_grad(in_pad, back_one, shape))
    pulled = transpose_part(first_pad, kernel_again(kernel_one), shape)
    input_grad = pulled.astype(jnp.bfloat16).reshape(inputs.shape)
    return (prediction, input_grad, grad_one, grad_two)


def solution(mesh):
    in_specs = (
        P("dp", None, "space", None, None),
        P("dp", None, "space", None),
        P("dp", None, None),
        P("dp", None, None),
        P("dp", None, "space", None, None),
    )
    out_specs = (
        P("dp", None, "space", None, None),
        P("dp", None, "space", None, None),
        P("dp", None, None),
        P("dp", None, None),
    )
    return jax.shard_map(
        on_device, mesh=mesh, in_specs=in_specs, out_specs=out_specs, check_vma=False
    )
```

profile of v0, /device:TPU:1, one launch (start us, length us, event | category | flops | bytes accessed | tf_op | source)
XLA Modules:
  0.0 553.1 jit_solution(8356080933103198237)
XLA Ops:
  7.9 1.1 multiply_convert_fusion
  9.0 5.4 collective-permute-start.4
  14.4 4.7 collective-permute-start.5
  19.1 0.9 fusion.31
  20.1 1.9 collective-permute-start
  22.0 2.4 collective-permute-start.1
  24.4 0.9 convert_element_type.54
  25.3 0.9 convert_element_type.56
  26.2 31.4 %all_gather.9 = bf16[128,27,128]{2,0,1:T(8,128)(2,1)S(1)} all-gather(bf16[8,27,128]{2,0,1:T(8,128)(2,1)S(1)} %convert_element_type.56), channel_id=1, replica_groups=mesh['dp'=16,'space'=32] {'dp'}, dimensions={0}, use_global_device_ids=true | all-gather | bytes 940032 | tf_op jit(solution)/shard_map/all_gather | solution.py:86
  57.7 28.5 %all_gather.8 = bf16[128,27,128]{2,0,1:T(8,128)(2,1)S(1)} all-gather(bf16[8,27,128]{2,0,1:T(8,128)(2,1)S(1)} %convert_element_type.54), channel_id=1, replica_groups=mesh['dp'=16,'space'=32] {'dp'}, dimensions={0}, use_global_device_ids=true | all-gather | bytes 940032 | tf_op jit(solution)/shard_map/all_gather | solution.py:86
  86.4 0.9 copy.69
  87.5 0.9 copy.67
  88.4 0.9 copy.72
  89.3 0.9 copy.71
  90.2 0.9 copy.70
  103.9 17.2 %collective-permute-start.2 = (bf16[1,10,1,32,128]{4,3,2,1,0:T(8,128)(2,1)S(1)}, bf16[1,10,1,32,128]{4,3,2,1,0:T(8,128)(2,1)S(1)}, u32[]{:S(2)}, u32[]{:S(2)}) collective-permute-start(bf16[1,10,1,32,128]{4,3,2,1,0:T(8,128)(2,1)S(1)} %get-tuple-element.118), channel_id=1, source_target_pairs={{0,1},{1,2},{2,3},{3,4},{4,5},{5,6},{6,7},{7,8},{8,9},{9,10},{10,1... | collective-permute-start | bytes 245768 | tf_op jit(solution)/shard_map/ppermute | solution.py:15
  121.1 1.9 collective-permute-start.3
  123.1 1.3 pad_maximum_fusion
  124.5 3.6 collective-permute-start.6
  128.1 2.1 collective-permute-start.7
  131.7 1.5 fusion.24
  134.1 1.0 fusion.21
  135.1 1.8 fusion.20
  136.9 0.8 copy.53
  137.7 0.8 copy.52
  138.5 0.8 copy.51
  139.3 0.8 copy.50
  140.1 0.8 copy.49
  140.9 0.9 constant_dynamic-update-slice_fusion.35
  141.9 1.7 copy.66
  143.6 1.7 copy.65
  145.3 1.7 copy.64
  147.0 1.7 copy.63
  148.7 0.8 copy.62
  149.6 0.8 copy.61
  150.4 0.8 copy.60
  151.2 0.8 copy.59
  152.8 0.8 copy.57
  153.6 0.8 copy.56
  154.4 0.8 copy.55
  155.3 0.8 copy.54
  156.1 1.0 constant_dynamic-update-slice_fusion.53
  157.1 1.6 constant_dynamic-update-slice_fusion.44
  158.7 1.0 pad_maximum_fusion.6
  160.4 1.6 constant_dynamic-update-slice_fusion.42
  162.0 1.6 constant_dynamic-update-slice_fusion.41
  167.2 3.7 copy.73
  170.8 1.7 constant_dynamic-update-slice_fusion.89
  172.5 1.6 constant_dynamic-update-slice_fusion.107
  174.2 1.6 pad_maximum_fusion.2
  180.5 1.4 pad_maximum_fusion.1
  182.0 1.8 constant_dynamic-update-slice_fusion.88
  183.8 1.7 constant_dynamic-update-slice_fusion.87
  185.5 1.7 constant_dynamic-update-slice_fusion.86
  187.1 1.7 constant_dynamic-update-slice_fusion.85
  188.8 1.7 constant_dynamic-update-slice_fusion.84
  190.5 1.6 constant_dynamic-update-slice_fusion.83
  196.6 2.0 convolution_add_fusion.5
  198.6 1.3 fusion.5
  200.5 68.5 %reduce-scatter.5.cloned.1.call-done = f32[8,27,128]{2,0,1:T(8,128)} async-done(((f32[128,27,128]{2,0,1:T(8,128)}), f32[8,27,128]{2,0,1:T(8,128)}) %reduce-scatter.5.cloned.1.call-update) | async-done | bytes 110608 | tf_op jit(solution)/shard_map/reduce_scatter | solution.py:90
  269.0 1.2 fusion.6
  270.2 273.3 %all-reduce.7.cloned.1.call-done = (f32[8,27,128]{2,0,1:T(8,128)}, f32[8,27,128]{2,0,1:T(8,128)}) async-done(((f32[8,27,128]{2,0,1:T(8,128)}, f32[8,27,128]{2,0,1:T(8,128)}), (f32[8,27,128]{2,0,1:T(8,128)}, f32[8,27,128]{2,0,1:T(8,128)})) %all-reduce.7.cloned.1.call-update) | async-done | bytes 221200 | tf_op jit(solution)/shard_map/psum | solution.py:91
  543.5 1.5 copy.172
  545.0 1.5 copy.173
  (277 shorter events, 30.2 us)
Async XLA Ops:
  7.2 193.3 %reduce-scatter.3.cloned.1.call-start = ((), (), s32[]{:S(2)}) async-start(), calls=%async_computation.2 | async-start | bytes 1880064 | tf_op jit(solution)/shard_map/reduce_scatter | solution.py:90
  9.0 83.1 %collective-permute-start.4 = (bf16[1,10,1,32,128]{4,3,2,1,0:T(8,128)(2,1)S(1)}, bf16[1,10,1,32,128]{4,3,2,1,0:T(8,128)(2,1)S(1)}, u32[]{:S(2)}, u32[]{:S(2)}) collective-permute-start(bf16[1,10,1,32,128]{4,3,2,1,0:T(8,128)(2,1)S(1)} %get-tuple-element.114), channel_id=1, source_target_pairs={{0,1},{1,2},{2,3},{3,4},{4,5},{5,6},{6,7},{7,8},{8,9},{9,10},{10,1... | collective-permute-start | bytes 245768 | tf_op jit(solution)/shard_map/ppermute | solution.py:15
  14.4 77.7 %collective-permute-start.5 = (bf16[1,10,1,32,128]{4,3,2,1,0:T(8,128)(2,1)S(1)}, bf16[1,10,1,32,128]{4,3,2,1,0:T(8,128)(2,1)S(1)}, u32[]{:S(2)}, u32[]{:S(2)}) collective-permute-start(bf16[1,10,1,32,128]{4,3,2,1,0:T(8,128)(2,1)S(1)} %get-tuple-element.115), channel_id=1, source_target_pairs={{1,0},{2,1},{3,2},{4,3},{5,4},{6,5},{7,6},{8,7},{9,8},{10,9},{11,1... | collective-permute-start | bytes 245768 | tf_op jit(solution)/shard_map/ppermute | solution.py:17
  20.1 71.1 %collective-permute-start = (bf16[1,10,1,32,128]{4,3,2,1,0:T(8,128)(2,1)S(1)}, bf16[1,10,1,32,128]{4,3,2,1,0:T(8,128)(2,1)S(1)}, u32[]{:S(2)}, u32[]{:S(2)}) collective-permute-start(bf16[1,10,1,32,128]{4,3,2,1,0:T(8,128)(2,1)S(1)} %get-tuple-element.122), channel_id=1, source_target_pairs={{0,1},{1,2},{2,3},{3,4},{4,5},{5,6},{6,7},{7,8},{8,9},{9,10},{10,1... | collective-permute-start | bytes 245768 | tf_op jit(solution)/shard_map/ppermute | solution.py:15
  22.0 69.1 %collective-permute-start.1 = (bf16[1,10,1,32,128]{4,3,2,1,0:T(8,128)(2,1)S(1)}, bf16[1,10,1,32,128]{4,3,2,1,0:T(8,128)(2,1)S(1)}, u32[]{:S(2)}, u32[]{:S(2)}) collective-permute-start(bf16[1,10,1,32,128]{4,3,2,1,0:T(8,128)(2,1)S(1)} %get-tuple-element.123), channel_id=1, source_target_pairs={{1,0},{2,1},{3,2},{4,3},{5,4},{6,5},{7,6},{8,7},{9,8},{10,9},{11,1... | collective-permute-start | bytes 245768 | tf_op jit(solution)/shard_map/ppermute | solution.py:17
  57.6 29.6 %copy-start.1 = (bf16[128,9,128]{2,0,1:T(8,128)(2,1)}, bf16[128,9,128]{2,0,1:T(8,128)(2,1)S(1)}, u32[]{:S(2)}) copy-start(bf16[128,9,128]{2,0,1:T(8,128)(2,1)S(1)} %get-tuple-element.6) | copy-start | bytes 884740
  57.7 29.6 %copy-start.3 = (bf16[128,9,128]{2,0,1:T(8,128)(2,1)}, bf16[128,9,128]{2,0,1:T(8,128)(2,1)S(1)}, u32[]{:S(2)}) copy-start(bf16[128,9,128]{2,0,1:T(8,128)(2,1)S(1)} %get-tuple-element.7) | copy-start | bytes 884740
  57.7 29.8 %copy-start.5 = (bf16[128,9,128]{2,0,1:T(8,128)(2,1)}, bf16[128,9,128]{2,0,1:T(8,128)(2,1)S(1)}, u32[]{:S(2)}) copy-start(bf16[128,9,128]{2,0,1:T(8,128)(2,1)S(1)} %get-tuple-element.8) | copy-start | bytes 884740
  86.3 3.9 copy-start.16
  87.3 3.9 copy-start.7
  103.9 26.3 %collective-permute-start.2 = (bf16[1,10,1,32,128]{4,3,2,1,0:T(8,128)(2,1)S(1)}, bf16[1,10,1,32,128]{4,3,2,1,0:T(8,128)(2,1)S(1)}, u32[]{:S(2)}, u32[]{:S(2)}) collective-permute-start(bf16[1,10,1,32,128]{4,3,2,1,0:T(8,128)(2,1)S(1)} %get-tuple-element.118), channel_id=1, source_target_pairs={{0,1},{1,2},{2,3},{3,4},{4,5},{5,6},{6,7},{7,8},{8,9},{9,10},{10,1... | collective-permute-start | bytes 245768 | tf_op jit(solution)/shard_map/ppermute | solution.py:15
  121.1 9.1 %collective-permute-start.3 = (bf16[1,10,1,32,128]{4,3,2,1,0:T(8,128)(2,1)S(1)}, bf16[1,10,1,32,128]{4,3,2,1,0:T(8,128)(2,1)S(1)}, u32[]{:S(2)}, u32[]{:S(2)}) collective-permute-start(bf16[1,10,1,32,128]{4,3,2,1,0:T(8,128)(2,1)S(1)} %get-tuple-element.119), channel_id=1, source_target_pairs={{1,0},{2,1},{3,2},{4,3},{5,4},{6,5},{7,6},{8,7},{9,8},{10,9},{11,1... | collective-permute-start | bytes 245768 | tf_op jit(solution)/shard_map/ppermute | solution.py:17
  124.4 144.5 %reduce-scatter.5.cloned.1.call-start = ((), (), s32[]{:S(2)}) async-start(), calls=%async_computation.3 | async-start | bytes 1880064 | tf_op jit(solution)/shard_map/reduce_scatter | solution.py:90
  124.5 8.9 %collective-permute-start.6 = (bf16[1,10,1,32,128]{4,3,2,1,0:T(8,128)(2,1)S(1)}, bf16[1,10,1,32,128]{4,3,2,1,0:T(8,128)(2,1)S(1)}, u32[]{:S(2)}, u32[]{:S(2)}) collective-permute-start(bf16[1,10,1,32,128]{4,3,2,1,0:T(8,128)(2,1)S(1)} %get-tuple-element.110), channel_id=1, source_target_pairs={{0,1},{1,2},{2,3},{3,4},{4,5},{5,6},{6,7},{7,8},{8,9},{9,10},{10,1... | collective-permute-start | bytes 245768 | tf_op jit(solution)/shard_map/ppermute | solution.py:15
  128.1 5.8 %collective-permute-start.7 = (bf16[1,10,1,32,128]{4,3,2,1,0:T(8,128)(2,1)S(1)}, bf16[1,10,1,32,128]{4,3,2,1,0:T(8,128)(2,1)S(1)}, u32[]{:S(2)}, u32[]{:S(2)}) collective-permute-start(bf16[1,10,1,32,128]{4,3,2,1,0:T(8,128)(2,1)S(1)} %get-tuple-element.111), channel_id=1, source_target_pairs={{1,0},{2,1},{3,2},{4,3},{5,4},{6,5},{7,6},{8,7},{9,8},{10,9},{11,1... | collective-permute-start | bytes 245768 | tf_op jit(solution)/shard_map/ppermute | solution.py:17
  133.9 3.0 copy-start.62
  156.1 8.2 %copy-start.37 = (bf16[1,10,2,32,128]{4,3,2,1,0:T(8,128)(2,1)S(1)}, bf16[1,10,2,32,128]{4,3,2,1,0:T(8,128)(2,1)}, u32[]{:S(2)}) copy-start(bf16[1,10,2,32,128]{4,3,2,1,0:T(8,128)(2,1)} %get-tuple-element.71) | copy-start | bytes 491524
  156.1 8.9 %copy-start.35 = (bf16[1,10,2,32,128]{4,3,2,1,0:T(8,128)(2,1)S(1)}, bf16[1,10,2,32,128]{4,3,2,1,0:T(8,128)(2,1)}, u32[]{:S(2)}) copy-start(bf16[1,10,2,32,128]{4,3,2,1,0:T(8,128)(2,1)} %get-tuple-element.70) | copy-start | bytes 491524
  158.7 7.8 %copy-start.33 = (bf16[1,10,2,32,128]{4,3,2,1,0:T(8,128)(2,1)S(1)}, bf16[1,10,2,32,128]{4,3,2,1,0:T(8,128)(2,1)}, u32[]{:S(2)}) copy-start(bf16[1,10,2,32,128]{4,3,2,1,0:T(8,128)(2,1)} %get-tuple-element.69) | copy-start | bytes 491524
  167.2 7.0 %copy-start.38 = (bf16[1,10,2,32,128]{4,3,2,1,0:T(8,128)(2,1)S(1)}, bf16[1,10,2,32,128]{4,3,2,1,0:T(8,128)(2,1)}, u32[]{:S(2)}) copy-start(bf16[1,10,2,32,128]{4,3,2,1,0:T(8,128)(2,1)} %get-tuple-element.26) | copy-start | bytes 491524
  170.8 5.1 copy-start.36
  170.8 5.1 copy-start.34
  170.8 5.3 copy-start.51
  172.5 3.6 copy-start.49
  174.2 2.0 copy-start.47
  174.2 2.1 copy-start.45
  175.9 1.0 copy-start.53
  176.0 1.2 copy-start.52
  176.0 1.3 copy-start.50
  176.1 1.5 copy-start.8
  176.1 1.4 copy-start.48
  176.2 1.6 copy-start.46
  176.2 1.6 copy-start.44
  176.3 1.6 copy-start.43
  176.8 1.2 copy-start.42
  176.8 1.1 copy-start.41
  176.9 1.1 copy-start.40
  178.6 1.4 copy-start
  181.9 10.2 %copy-start.32 = (bf16[1,10,2,32,128]{4,3,2,1,0:T(8,128)(2,1)S(1)}, bf16[1,10,2,32,128]{4,3,2,1,0:T(8,128)(2,1)}, u32[]{:S(2)}) copy-start(bf16[1,10,2,32,128]{4,3,2,1,0:T(8,128)(2,1)} %get-tuple-element.28) | copy-start | bytes 491524
  181.9 10.9 %copy-start.31 = (bf16[1,10,2,32,128]{4,3,2,1,0:T(8,128)(2,1)S(1)}, bf16[1,10,2,32,128]{4,3,2,1,0:T(8,128)(2,1)}, u32[]{:S(2)}) copy-start(bf16[1,10,2,32,128]{4,3,2,1,0:T(8,128)(2,1)} %get-tuple-element.27) | copy-start | bytes 491524
  181.9 11.6 %copy-start.30 = (bf16[1,10,2,32,128]{4,3,2,1,0:T(8,128)(2,1)S(1)}, bf16[1,10,2,32,128]{4,3,2,1,0:T(8,128)(2,1)}, u32[]{:S(2)}) copy-start(bf16[1,10,2,32,128]{4,3,2,1,0:T(8,128)(2,1)} %get-tuple-element.19) | copy-start | bytes 491524
  181.9 361.5 %all-reduce.7.cloned.1.call-start = ((), (), s32[]{:S(2)}) async-start(), calls=%async_computation.4 | async-start | bytes 442368 | tf_op jit(solution)/shard_map/psum | solution.py:91
  182.0 11.5 %copy-start.10 = (bf16[640,1152]{1,0:T(8,128)(2,1)S(1)}, bf16[640,1152]{1,0:T(8,128)(2,1)}, u32[]{:S(2)}) copy-start(bf16[640,1152]{1,0:T(8,128)(2,1)} %constant_dynamic-update-slice_fusion.107) | copy-start | bytes 4423684
  182.0 11.6 %copy-start.29 = (bf16[1,10,2,32,128]{4,3,2,1,0:T(8,128)(2,1)S(1)}, bf16[1,10,2,32,128]{4,3,2,1,0:T(8,128)(2,1)}, u32[]{:S(2)}) copy-start(bf16[1,10,2,32,128]{4,3,2,1,0:T(8,128)(2,1)} %get-tuple-element.18) | copy-start | bytes 491524
  183.8 9.9 %copy-start.28 = (bf16[1,10,2,32,128]{4,3,2,1,0:T(8,128)(2,1)S(1)}, bf16[1,10,2,32,128]{4,3,2,1,0:T(8,128)(2,1)}, u32[]{:S(2)}) copy-start(bf16[1,10,2,32,128]{4,3,2,1,0:T(8,128)(2,1)} %get-tuple-element.17) | copy-start | bytes 491524
  185.5 8.2 %copy-start.27 = (bf16[1,10,2,32,128]{4,3,2,1,0:T(8,128)(2,1)S(1)}, bf16[1,10,2,32,128]{4,3,2,1,0:T(8,128)(2,1)}, u32[]{:S(2)}) copy-start(bf16[1,10,2,32,128]{4,3,2,1,0:T(8,128)(2,1)} %get-tuple-element.16) | copy-start | bytes 491524
  187.1 6.7 %copy-start.26 = (bf16[1,10,2,32,128]{4,3,2,1,0:T(8,128)(2,1)S(1)}, bf16[1,10,2,32,128]{4,3,2,1,0:T(8,128)(2,1)}, u32[]{:S(2)}) copy-start(bf16[1,10,2,32,128]{4,3,2,1,0:T(8,128)(2,1)} %get-tuple-element.15) | copy-start | bytes 491524
  188.8 5.0 copy-start.25
  190.5 3.4 copy-start.24
  192.1 1.8 copy-start.23
  192.8 1.5 copy-start.9
  192.8 1.5 copy-start.22
  193.5 1.0 copy-start.21
  193.6 1.0 copy-start.39
  193.7 1.0 copy-start.20
  193.7 1.1 copy-start.6
  194.0 1.4 copy-start.11
  194.6 1.4 copy-start.13
  194.6 1.4 copy-start.18
  195.5 1.2 copy-start.4
  196.6 2.0 copy-start.2
  198.6 1.3 copy-start.15
  199.9 69.1 %copy-start.12 = (bf16[640,1152]{1,0:T(8,128)(2,1)S(1)}, bf16[640,1152]{1,0:T(8,128)(2,1)}, u32[]{:S(2)}) copy-start(bf16[640,1152]{1,0:T(8,128)(2,1)} %copy-done.11) | copy-start | bytes 4423684
  199.9 69.1 %copy-start.14 = (bf16[128,9,128]{0,2,1:T(8,128)(2,1)S(1)}, bf16[128,9,128]{0,2,1:T(8,128)(2,1)}, u32[]{:S(2)}) copy-start(bf16[128,9,128]{0,2,1:T(8,128)(2,1)} %copy.72) | copy-start | bytes 884740
  (13 other events, 11.0 us)
Sparse Core Ops, SparseCore 0:
  124.5 69.2 reduce-scatter.2
  196.9 72.0 reduce-scatter.4
  271.9 271.5 all-reduce.6
where the time goes:
time: 554 us; the launch traced here: 553 us
  waiting for transfers between devices  342 us (62%)
  local copies, waits for them, and re-layouts  73.7 us (13%)
  blocking collectives  59.9 us (11%)
  starting transfers between devices  39.4 us (7%)
  between operations  15.2 us (3%)
  matrix products  13 us (2%)
  other arithmetic  9.63 us (2%)
    psum x1, waiting for transfers between devices, reduce_grad(): return lax.psum(owned, 'space')  273 us
    reduce_scatter x2, waiting for transfers between devices, reduce_grad(): owned = lax.psum_scatter(grad_full, 'dp', scatter_dimension=0, tiled=True)  68.5 us
    all_gather x2, blocking collectives, kernel_again(): return lax.all_gather(kernel, 'dp', axis=0, tiled=True)  59.9 us
    unnamed x230, local copies, waits for them, and re-layouts  38.1 us
    ppermute x4, starting transfers between devices, with_halo(): lax.ppermute(tail, axis, [(i, (i + 1) % count) for i in range(ends)])  28.2 us
    reshape x18, local copies, waits for them, and re-layouts, group_window(): pieces.append(piece.reshape(-1, padded.shape[4]))  18.3 us
    ppermute x4, starting transfers between devices, with_halo(): lax.ppermute(head, axis, [((i + 1) % count, i) for i in range(ends)])  11.1 us
  transfers between devices with their start and end apart: 11, of which 3 were waited for; matrix products, arithmetic and copies ran while one was open for 14% of the time, Pallas kernels for 0%

commit v1 on v0

v1 whole, which is shorter than its diff:
```python
import jax
import jax.numpy as jnp
from jax import lax
from jax.sharding import PartitionSpec as P

HALO = 2
SPATIAL = ("NDHWC", "DHWIO", "NDHWC")


def exchange_rows(cells, width):
    count = lax.axis_size("space")
    ends = count - 1
    rows = cells.shape[2]
    head = lax.slice_in_dim(cells, 0, width, axis=2)
    tail = lax.slice_in_dim(cells, rows - width, rows, axis=2)
    above = lax.ppermute(tail, "space", [(i, i + 1) for i in range(ends)])
    below = lax.ppermute(head, "space", [(i + 1, i) for i in range(ends)])
    return jnp.concatenate([above, cells, below], axis=2)


def pad_depth_cols(field):
    return jnp.pad(field, ((0, 0), (1, 1), (0, 0), (1, 1), (0, 0)))


def conv(padded, kernel):
    return lax.conv_general_dilated(
        padded, kernel, (1, 1, 1), "VALID", dimension_numbers=SPATIAL,
        preferred_element_type=jnp.float32,
    )


def weight_grad(padded, back):
    out = lax.conv_general_dilated(
        padded, back, (1, 1, 1), "VALID", dimension_numbers=("CDHWN", "IDHWO", "NDHWC"),
        preferred_element_type=jnp.float32,
    )
    return out.reshape(out.shape[0], 27, out.shape[4])


def gather_kernel(weight):
    count = lax.axis_size("dp")
    local = weight.astype(jnp.bfloat16)
    copies = jnp.broadcast_to(local[None], (count,) + local.shape)
    full = lax.all_to_all(copies, "dp", 0, 0).reshape((-1,) + local.shape[1:])
    channel = full.shape[0]
    forward = jnp.transpose(full.reshape(channel, 3, 3, 3, full.shape[2]), (1, 2, 3, 0, 4))
    backward = jnp.transpose(forward[::-1, ::-1, ::-1], (0, 1, 2, 4, 3))
    return forward, backward


def reduce_grad(grad_full):
    count = lax.axis_size("dp")
    parts = grad_full.reshape((count, -1) + grad_full.shape[1:])
    owned = lax.all_to_all(parts, "dp", 0, 0).sum(axis=0)
    size = lax.axis_size("space")
    step = 1
    while step < size:
        owned = owned + lax.ppermute(owned, "space", [(i, i ^ step) for i in range(size)])
        step *= 2
    return owned


def on_device(inputs, land_mask, weight_one, weight_two, cotangent):
    rows = inputs.shape[2]
    channel = inputs.shape[4]
    mask = land_mask.astype(jnp.bfloat16)[..., None]
    back_two = (cotangent.astype(jnp.float32) * mask.astype(jnp.float32)).astype(jnp.bfloat16)
    both = exchange_rows(jnp.concatenate([inputs, back_two], axis=4), HALO)
    mask_wide = exchange_rows(mask, HALO).astype(jnp.float32)
    in_wide = both[..., :channel]
    back_two_wide = both[..., channel:]
    mask_mid = mask_wide[:, :, 1 : rows + 3]
    mask_own = mask_wide[:, :, 2 : rows + 2]

    k1, k1_t = gather_kernel(weight_one)
    k2, k2_t = gather_kernel(weight_two)

    pre_one = conv(pad_depth_cols(in_wide), k1)
    sigma = jax.nn.sigmoid(pre_one)
    act_one = (mask_mid * (pre_one * sigma)).astype(jnp.bfloat16)
    act_pad = pad_depth_cols(act_one)
    prediction = (mask_own * conv(act_pad, k2)).astype(jnp.bfloat16)

    back_own = back_two_wide[:, :, HALO : HALO + rows]
    grad_two = reduce_grad(weight_grad(act_pad, back_own))

    pull_one = conv(pad_depth_cols(back_two_wide), k2_t)
    back_one = (pull_one * mask_mid * sigma * (1.0 + pre_one * (1.0 - sigma))).astype(jnp.bfloat16)
    in_mid = pad_depth_cols(in_wide[:, :, 1 : rows + 3])
    grad_one = reduce_grad(weight_grad(in_mid, back_one[:, :, 1 : rows + 1]))
    input_grad = conv(pad_depth_cols(back_one), k1_t).astype(jnp.bfloat16)
    return (prediction, input_grad, grad_one, grad_two)


def solution(mesh):
    in_specs = (
        P("dp", None, "space", None, None),
        P("dp", None, "space", None),
        P("dp", None, None),
        P("dp", None, None),
        P("dp", None, "space", None, None),
    )
    out_specs = (
        P("dp", None, "space", None, None),
        P("dp", None, "space", None, None),
        P("dp", None, None),
        P("dp", None, None),
    )
    return jax.shard_map(
        on_device, mesh=mesh, in_specs=in_specs, out_specs=out_specs, check_vma=False
    )
```

time: 554 us -> 227 us (0.41)
  waiting for transfers between devices: 342 us -> 88.6 us
  blocking collectives: 59.9 us -> 0 us
  local copies, waits for them, and re-layouts: 73.7 us -> 22.3 us
  starting transfers between devices: 39.4 us -> 80.9 us
  between operations: 15.2 us -> 1.44 us
  matrix products: 13 us -> 20.2 us
    psum x1 -> x0, waiting for transfers between devices: 273 us -> none  [reduce_grad(): return lax.psum(owned, 'space')]
    all_to_all x0 -> x4, waiting for transfers between devices: none -> 81.4 us  [the longest x2 72.4 us: reduce_grad(): owned = lax.all_to_all(parts, 'dp', 0, 0).sum(axis=0)]
    reduce_scatter x2 -> x0, waiting for transfers between devices: 68.5 us -> none  [reduce_grad(): owned = lax.psum_scatter(grad_full, 'dp', scatter_dimension=0, tiled=True)]
    all_gather x2 -> x0, blocking collectives: 59.9 us -> none  [kernel_again(): return lax.all_gather(kernel, 'dp', axis=0, tiled=True)]
    unnamed x230 -> x46, local copies, waits for them, and re-layouts: 38.1 us -> 4.47 us
    all_to_all x0 -> x4, starting transfers between devices: none -> 26.9 us  [the longest x2 16.6 us: gather_kernel(): full = lax.all_to_all(copies, 'dp', 0, 0).reshape((-1,) + local.shape[1:])]
    conv_general_dilated x0 -> x6, matrix products: none -> 20.2 us  [the longest x2 10.5 us: weight_grad(): lax.conv_general_dilated(padded, back, (1, 1, 1), 'VALID', dimension_numb...]
    reshape x18 -> x0, local copies, waits for them, and re-layouts: 18.3 us -> none  [group_window(): pieces.append(piece.reshape(-1, padded.shape[4]))]
  transfers between devices with their start and end apart: 11 -> 18, of which waited for: 3 -> 7; matrix products, arithmetic and copies ran while one was open for 14% -> 16% of each run, Pallas kernels for 0% -> 0%
where the time goes in v1:
time: 227 us; the launch traced here: 224 us
  waiting for transfers between devices  88.6 us (39%)
  starting transfers between devices  80.9 us (36%)
  local copies, waits for them, and re-layouts  22.3 us (10%)
  matrix products  20.2 us (9%)
  other arithmetic  10.9 us (5%)
    all_to_all x2, waiting for transfers between devices, reduce_grad(): owned = lax.all_to_all(parts, 'dp', 0, 0).sum(axis=0)  72.4 us
    ppermute x10, starting transfers between devices, reduce_grad(): lax.ppermute(owned, 'space', [(i, i ^ step) for i in range(size)])  41.6 us
    all_to_all x2, starting transfers between devices, gather_kernel(): full = lax.all_to_all(copies, 'dp', 0, 0).reshape((-1,) + local.shape[1:])  16.6 us
    conv_general_dilated x2, matrix products, weight_grad(): lax.conv_general_dilated(padded, back, (1, 1, 1), 'VALID', dimension_numb...  10.5 us
    all_to_all x2, starting transfers between devices, reduce_grad(): owned = lax.all_to_all(parts, 'dp', 0, 0).sum(axis=0)  10.3 us
    conv_general_dilated x4, matrix products, conv(): lax.conv_general_dilated(padded, kernel, (1, 1, 1), 'VALID', dimension_nu...  9.67 us
    all_to_all x2, waiting for transfers between devices, gather_kernel(): full = lax.all_to_all(copies, 'dp', 0, 0).reshape((-1,) + local.shape[1:])  9.01 us
    ppermute x2, starting transfers between devices, exchange_rows(): above = lax.ppermute(tail, 'space', [(i, i + 1) for i in range(ends)])  8.48 us
  transfers between devices with their start and end apart: 18, of which 7 were waited for; matrix products, arithmetic and copies ran while one was open for 16% of the time, Pallas kernels for 0%

profile of v1, /device:TPU:1, one launch (start us, length us, event | category | flops | bytes accessed | tf_op | source)
XLA Modules:
  0.0 224.2 jit_solution(4538170790897254251)
XLA Ops:
  0.7 0.9 convert_element_type.62
  1.6 1.0 broadcast_in_dim.7
  2.7 8.7 %all-to-all-start = ((bf16[16,8,27,128]{3,1,2,0:T(8,128)(2,1)}), bf16[16,8,27,128]{3,1,2,0:T(8,128)(2,1)S(1)}, u32[]{:S(2)}, u32[]{:S(2)}) async-start(bf16[16,8,27,128]{3,1,2,0:T(8,128)(2,1)} %broadcast_in_dim.7), calls=%async_computation | async-start | bytes 1769472 | tf_op jit(solution)/shard_map/all_to_all | solution.py:44
  11.4 0.3 copy.40
  11.7 0.8 fusion.40
  12.6 1.1 pad_maximum_fusion.1
  13.8 4.8 %collective-permute-start.2 = (bf16[1,10,2,32,256]{4,3,2,1,0:T(8,128)(2,1)S(1)}, bf16[1,10,2,32,256]{4,3,2,1,0:T(8,128)(2,1)S(1)}, u32[]{:S(2)}, u32[]{:S(2)}) collective-permute-start(bf16[1,10,2,32,256]{4,3,2,1,0:T(8,128)(2,1)S(1)} %copy.41), channel_id=1, source_target_pairs={{0,1},{1,2},{2,3},{3,4},{4,5},{5,6},{6,7},{7,8},{8,9},{9,10},{10,1... | collective-permute-start | bytes 983048 | tf_op jit(solution)/shard_map/ppermute | solution.py:16
  18.6 1.9 collective-permute-start.3
  20.6 3.6 %collective-permute-start = (bf16[1,10,2,32,1]{3,2,1,4,0:T(2,128)(2,1)S(1)}, bf16[1,10,2,32,1]{3,2,1,4,0:T(2,128)(2,1)S(1)}, u32[]{:S(2)}, u32[]{:S(2)}) collective-permute-start(bf16[1,10,2,32,1]{3,2,1,4,0:T(2,128)(2,1)S(1)} %get-tuple-element.19), channel_id=1, source_target_pairs={{0,1},{1,2},{2,3},{3,4},{4,5},{5,6},{6,7},{7,8},{8,9},{9,10},{10,1... | collective-permute-start | bytes 3848 | tf_op jit(solution)/shard_map/ppermute | solution.py:16
  24.2 1.9 collective-permute-start.1
  26.2 3.3 %collective-permute-done.1 = bf16[1,10,2,32,1]{3,2,1,4,0:T(2,128)(2,1)S(1)} collective-permute-done((bf16[1,10,2,32,1]{3,2,1,4,0:T(2,128)(2,1)S(1)}, bf16[1,10,2,32,1]{3,2,1,4,0:T(2,128)(2,1)S(1)}, u32[]{:S(2)}, u32[]{:S(2)}) %collective-permute-start.1) | collective-permute-done | bytes 1312 | tf_op jit(solution)/shard_map/ppermute | solution.py:17
  29.5 0.8 copy.38
  30.3 1.5 copy.43
  31.8 1.5 copy.44
  33.3 1.0 broadcast_in_dim.8
  34.3 7.9 %all-to-all-start.1 = ((bf16[16,8,27,128]{3,1,2,0:T(8,128)(2,1)}), bf16[16,8,27,128]{3,1,2,0:T(8,128)(2,1)}, u32[]{:S(2)}, u32[]{:S(2)}) async-start(bf16[16,8,27,128]{3,1,2,0:T(8,128)(2,1)} %broadcast_in_dim.8), calls=%async_computation.1 | async-start | bytes 1769472 | tf_op jit(solution)/shard_map/all_to_all | solution.py:44
  42.2 3.8 %pad_maximum_fusion = bf16[1,10,6,32,256]{4,0,3,2,1:T(2,128)(2,1)S(1)} fusion(bf16[1,10,2,32,256]{4,0,3,2,1:T(2,128)(2,1)} %copy.44, bf16[1,10,2,32,128]{4,0,3,2,1:T(2,128)(2,1)S(1)} %fusion.40, bf16[1,10,2,32,128]{4,0,3,2,1:T(2,128)(2,1)S(1)} %copy.40, bf16[1,10,2,32,256]{4,0,3,2,1:T(2,128)(2,1)} %copy.43), kind=kLoop, calls=%fused_computation | loop fusion | flops 3932160 | bytes 1966080 | tf_op jit(solution)/shard_map/concatenate | solution.py:18
  46.0 2.3 %fusion.58 = (bf16[1,10,6,32,128]{4,0,3,2,1:T(2,128)(2,1)S(1)}, bf16[1,10,6,32,128]{4,0,3,2,1:T(2,128)(2,1)S(1)}) fusion(bf16[1,10,6,32,256]{4,0,3,2,1:T(2,128)(2,1)S(1)} %pad_maximum_fusion), kind=kLoop, calls=%fused_computation.78 | loop fusion | bytes 1966080 | tf_op jit(solution)/shard_map/slice | solution.py:71
  48.3 1.6 copy_bitcast_fusion
  49.9 0.2 pad.7.clone
  50.5 0.8 slice.44
  51.2 0.2 copy.48
  51.5 3.3 %add_divide_fusion = (f32[10,4,8,5,128]{4,2,3,1,0:T(8,128)S(1)}, f32[10,4,8,5,128]{4,2,3,1,0:T(8,128)S(1)}, f32[10,4,8,5,128]{4,2,3,1,0:T(8,128)S(1)}) fusion(bf16[128,3,3,3,128]{4,0,3,2,1:T(8,128)(2,1)S(1)} %bitcast.66, bf16[10,6,1,7,2,128]{5,3,4,1,0,2:T(8,128)(2,1)S(1)} %slice.39, bf16[10,6,1,8,5,128]{5,3,4,1,0,2:T(8,128)(2,1)S(1)} %copy.47, ...), kind=kOutput, calls=%fused_computation.23 | convolution fusion | flops 1325424640 | bytes 4171816 | tf_op jit(solution)/shard_map/conv_general_dilated | solution.py:26
  54.8 0.2 copy.58
  55.0 1.1 copy.59
  56.1 1.1 copy.49
  57.2 9.0 %all-to-all-done.1 = bf16[16,8,27,128]{3,1,2,0:T(8,128)(2,1)} async-done(((bf16[16,8,27,128]{3,1,2,0:T(8,128)(2,1)}), bf16[16,8,27,128]{3,1,2,0:T(8,128)(2,1)}, u32[]{:S(2)}, u32[]{:S(2)}) %all-to-all-start.1) | async-done | bytes 884768 | tf_op jit(solution)/shard_map/all_to_all | solution.py:44
  66.2 1.4 copy.52
  67.7 3.2 %convolution_select_fusion = f32[10,4,8,5,128]{4,2,3,1,0:T(8,128)S(1)} fusion(bf16[128,3,3,3,128]{4,0,3,2,1:T(8,128)(2,1)S(1)} %bitcast.68, bf16[10,6,1,7,2,128]{5,3,4,1,0,2:T(8,128)(2,1)S(1)} %copy-done.7, bf16[10,6,1,8,5,128]{5,3,4,1,0,2:T(8,128)(2,1)S(1)} %copy.56, pred[8,5]{0,1:T(8,128)(4,1)S(1)} %copy-done.19), kind=kOutput, calls=%fused_computation.4 | convolution fusion | flops 1323991040 | bytes 2533416 | tf_op jit(solution)/shard_map/conv_general_dilated | solution.py:26
  70.9 0.2 copy.57
  71.2 0.9 copy-done
  72.1 0.2 copy-done.1
  72.3 0.5 fusion.17
  72.8 5.7 %fusion.21 = f32[128,3,3,3,128]{4,0,3,2,1:T(8,128)S(1)} fusion(bf16[1,10,4,32,128]{4,2,3,1,0:T(4,128)(2,1)S(1)} %bitcast.65, bf16[1,10,2,32,128]{4,3,2,1,0:T(8,128)(2,1)S(1)} %copy-done.9, f32[10,2,32]{2,1,0:T(2,128)S(1)} %get-tuple-element.20), kind=kOutput, calls=%fused_computation.35 | convolution fusion | flops 517718016 | bytes 2263552 | tf_op jit(solution)/shard_map/conv_general_dilated | solution.py:33
  78.5 1.4 copy.67
  79.9 4.4 %all-to-all-start.3 = ((f32[16,8,27,128]{3,1,2,0:T(8,128)}), f32[16,8,27,128]{3,1,2,0:T(8,128)}, u32[]{:S(2)}, u32[]{:S(2)}) async-start(f32[16,8,27,128]{3,1,2,0:T(8,128)} %copy.67), calls=%async_computation.3 | async-start | bytes 3538944 | tf_op jit(solution)/shard_map/all_to_all | solution.py:54
  84.3 0.2 slice.51
  84.5 4.8 %fusion.19 = f32[128,3,3,3,128]{4,0,3,2,1:T(8,128)S(1)} fusion(bf16[1,10,6,32,256]{4,0,3,2,1:T(2,128)(2,1)S(1)} %pad_maximum_fusion, bf16[1,10,2,32,128]{4,2,3,1,0:T(2,128)(2,1)S(1)} %slice.51), kind=kOutput, calls=%fused_computation.33 | convolution fusion | flops 517472256 | bytes 2588672 | tf_op jit(solution)/shard_map/conv_general_dilated | solution.py:33
  89.3 1.3 copy.65
  90.6 35.9 %all-to-all-done.3 = f32[16,8,27,128]{3,1,2,0:T(8,128)} async-done(((f32[16,8,27,128]{3,1,2,0:T(8,128)}), f32[16,8,27,128]{3,1,2,0:T(8,128)}, u32[]{:S(2)}, u32[]{:S(2)}) %all-to-all-start.3) | async-done | bytes 1769504 | tf_op jit(solution)/shard_map/all_to_all | solution.py:54
  126.5 5.9 %all-to-all-start.2 = ((f32[16,8,27,128]{3,1,2,0:T(8,128)}), f32[16,8,27,128]{3,1,2,0:T(8,128)S(1)}, u32[]{:S(2)}, u32[]{:S(2)}) async-start(f32[16,8,27,128]{3,1,2,0:T(8,128)} %copy.65), calls=%async_computation.2 | async-start | bytes 3538944 | tf_op jit(solution)/shard_map/all_to_all | solution.py:54
  132.5 1.6 reduce_sum.19
  134.0 2.7 %collective-permute-start.9 = (f32[8,27,128]{2,0,1:T(8,128)S(1)}, f32[8,27,128]{2,0,1:T(8,128)S(1)}, u32[]{:S(2)}, u32[]{:S(2)}) collective-permute-start(f32[8,27,128]{2,0,1:T(8,128)S(1)} %reduce_sum.19), channel_id=1, source_target_pairs={{0,1},{1,0},{2,3},{3,2},{4,5},{5,4},{6,7},{7,6},{8,9},{9,8},{10,11... | collective-permute-start | bytes 331784 | tf_op jit(solution)/shard_map/ppermute | solution.py:58
  136.7 36.6 %all-to-all-done.2 = f32[16,8,27,128]{3,1,2,0:T(8,128)S(1)} async-done(((f32[16,8,27,128]{3,1,2,0:T(8,128)}), f32[16,8,27,128]{3,1,2,0:T(8,128)S(1)}, u32[]{:S(2)}, u32[]{:S(2)}) %all-to-all-start.2) | async-done | bytes 1769504 | tf_op jit(solution)/shard_map/all_to_all | solution.py:54
  173.4 4.5 %collective-permute-start.4 = (f32[8,27,128]{2,0,1:T(8,128)S(1)}, f32[8,27,128]{2,0,1:T(8,128)S(1)}, u32[]{:S(2)}, u32[]{:S(2)}) collective-permute-start(f32[8,27,128]{2,0,1:T(8,128)S(1)} %reduce_sum.18), channel_id=1, source_target_pairs={{0,1},{1,0},{2,3},{3,2},{4,5},{5,4},{6,7},{7,6},{8,9},{9,8},{10,11... | collective-permute-start | bytes 331784 | tf_op jit(solution)/shard_map/ppermute | solution.py:58
  178.5 4.0 %collective-permute-start.10 = (f32[8,27,128]{2,0,1:T(8,128)S(1)}, f32[8,27,128]{2,0,1:T(8,128)S(1)}, u32[]{:S(2)}, u32[]{:S(2)}) collective-permute-start(f32[8,27,128]{2,0,1:T(8,128)S(1)} %add.43), channel_id=1, source_target_pairs={{0,2},{1,3},{2,0},{3,1},{4,6},{5,7},{6,4},{7,5},{8,10},{9,11},{10,... | collective-permute-start | bytes 331784 | tf_op jit(solution)/shard_map/ppermute | solution.py:58
  182.5 1.9 collective-permute-start.5
  184.4 1.6 convolution_select_fusion.3
  186.4 6.6 %collective-permute-start.11 = (f32[8,27,128]{2,0,1:T(8,128)S(1)}, f32[8,27,128]{2,0,1:T(8,128)S(1)}, u32[]{:S(2)}, u32[]{:S(2)}) collective-permute-start(f32[8,27,128]{2,0,1:T(8,128)S(1)} %add.44), channel_id=1, source_target_pairs={{0,4},{1,5},{2,6},{3,7},{4,0},{5,1},{6,2},{7,3},{8,12},{9,13},{10,... | collective-permute-start | bytes 331784 | tf_op jit(solution)/shard_map/ppermute | solution.py:58
  193.0 2.6 %collective-permute-start.6 = (f32[8,27,128]{2,0,1:T(8,128)S(1)}, f32[8,27,128]{2,0,1:T(8,128)S(1)}, u32[]{:S(2)}, u32[]{:S(2)}) collective-permute-start(f32[8,27,128]{2,0,1:T(8,128)S(1)} %add.39), channel_id=1, source_target_pairs={{0,4},{1,5},{2,6},{3,7},{4,0},{5,1},{6,2},{7,3},{8,12},{9,13},{10,... | collective-permute-start | bytes 331784 | tf_op jit(solution)/shard_map/ppermute | solution.py:58
  195.6 1.6 fusion.2
  197.2 0.2 copy.53
  197.5 1.1 collective-permute-done.11
  198.5 5.7 %collective-permute-start.12 = (f32[8,27,128]{2,0,1:T(8,128)S(1)}, f32[8,27,128]{2,0,1:T(8,128)S(1)}, u32[]{:S(2)}, u32[]{:S(2)}) collective-permute-start(f32[8,27,128]{2,0,1:T(8,128)S(1)} %add.45), channel_id=1, source_target_pairs={{0,8},{1,9},{2,10},{3,11},{4,12},{5,13},{6,14},{7,15},{8,0},{9,1},... | collective-permute-start | bytes 331784 | tf_op jit(solution)/shard_map/ppermute | solution.py:58
  204.3 4.9 %collective-permute-start.7 = (f32[8,27,128]{2,0,1:T(8,128)S(1)}, f32[8,27,128]{2,0,1:T(8,128)S(1)}, u32[]{:S(2)}, u32[]{:S(2)}) collective-permute-start(f32[8,27,128]{2,0,1:T(8,128)S(1)} %add.40), channel_id=1, source_target_pairs={{0,8},{1,9},{2,10},{3,11},{4,12},{5,13},{6,14},{7,15},{8,0},{9,1},... | collective-permute-start | bytes 331784 | tf_op jit(solution)/shard_map/ppermute | solution.py:58
  209.2 0.4 fusion.43
  209.8 4.3 %collective-permute-start.13 = (f32[8,27,128]{2,0,1:T(8,128)S(1)}, f32[8,27,128]{2,0,1:T(8,128)S(1)}, u32[]{:S(2)}, u32[]{:S(2)}) collective-permute-start(f32[8,27,128]{2,0,1:T(8,128)S(1)} %add.46), channel_id=1, source_target_pairs={{0,16},{1,17},{2,18},{3,19},{4,20},{5,21},{6,22},{7,23},{8,24},{9,... | collective-permute-start | bytes 331784 | tf_op jit(solution)/shard_map/ppermute | solution.py:58
  214.1 2.3 %collective-permute-done.7 = f32[8,27,128]{2,0,1:T(8,128)S(1)} collective-permute-done((f32[8,27,128]{2,0,1:T(8,128)S(1)}, f32[8,27,128]{2,0,1:T(8,128)S(1)}, u32[]{:S(2)}, u32[]{:S(2)}) %collective-permute-start.7) | collective-permute-done | bytes 110624 | tf_op jit(solution)/shard_map/ppermute | solution.py:58
  216.5 4.4 %collective-permute-start.8 = (f32[8,27,128]{2,0,1:T(8,128)S(1)}, f32[8,27,128]{2,0,1:T(8,128)S(1)}, u32[]{:S(2)}, u32[]{:S(2)}) collective-permute-start(f32[8,27,128]{2,0,1:T(8,128)S(1)} %add.41), channel_id=1, source_target_pairs={{0,16},{1,17},{2,18},{3,19},{4,20},{5,21},{6,22},{7,23},{8,24},{9,... | collective-permute-start | bytes 331784 | tf_op jit(solution)/shard_map/ppermute | solution.py:58
  221.0 0.7 copy.69
  221.7 0.7 copy.68
  222.4 0.7 add.47
  223.1 0.4 collective-permute-done.8
  223.5 0.7 add.42
  (78 shorter events, 1.8 us)
Async XLA Ops:
  0.6 10.7 %copy-start.10 = (bf16[1,10,2,32,128]{4,3,2,1,0:T(8,128)(2,1)S(1)}, bf16[1,10,2,32,128]{4,3,2,1,0:T(8,128)(2,1)}, u32[]{:S(2)}) copy-start(bf16[1,10,2,32,128]{4,3,2,1,0:T(8,128)(2,1)} %param.5) | copy-start | bytes 491524
  0.6 11.0 %copy-start.18 = (s32[1,10,2,32]{3,2,1,0:T(2,128)S(1)}, s32[1,10,2,32]{3,2,1,0:T(2,128)}, u32[]{:S(2)}) copy-start(s32[1,10,2,32]{3,2,1,0:T(2,128)} %param.6) | copy-start | bytes 7684
  0.7 11.1 %copy-start.8 = (bf16[1,10,2,32,128]{4,3,2,1,0:T(8,128)(2,1)S(1)}, bf16[1,10,2,32,128]{4,3,2,1,0:T(8,128)(2,1)}, u32[]{:S(2)}) copy-start(bf16[1,10,2,32,128]{4,3,2,1,0:T(8,128)(2,1)} %param.9) | copy-start | bytes 491524
  2.7 30.6 %all-to-all-start = ((bf16[16,8,27,128]{3,1,2,0:T(8,128)(2,1)}), bf16[16,8,27,128]{3,1,2,0:T(8,128)(2,1)S(1)}, u32[]{:S(2)}, u32[]{:S(2)}) async-start(bf16[16,8,27,128]{3,1,2,0:T(8,128)(2,1)} %broadcast_in_dim.7), calls=%async_computation | async-start | bytes 1769472 | tf_op jit(solution)/shard_map/all_to_all | solution.py:44
  11.4 14.8 %copy-start.11 = (f32[8,27,128]{2,0,1:T(8,128)S(1)}, f32[8,27,128]{2,0,1:T(8,128)}, u32[]{:S(2)}) copy-start(f32[8,27,128]{2,0,1:T(8,128)} %param.8) | copy-start | bytes 331780
  11.7 20.1 %copy-start.12 = (bf16[1,10,2,32,1]{3,2,1,4,0:T(2,128)(2,1)}, bf16[1,10,2,32,1]{3,2,1,4,0:T(2,128)(2,1)S(1)}, u32[]{:S(2)}) copy-start(bf16[1,10,2,32,1]{3,2,1,4,0:T(2,128)(2,1)S(1)} %get-tuple-element.19) | copy-start | bytes 3844
  13.8 16.5 %collective-permute-start.2 = (bf16[1,10,2,32,256]{4,3,2,1,0:T(8,128)(2,1)S(1)}, bf16[1,10,2,32,256]{4,3,2,1,0:T(8,128)(2,1)S(1)}, u32[]{:S(2)}, u32[]{:S(2)}) collective-permute-start(bf16[1,10,2,32,256]{4,3,2,1,0:T(8,128)(2,1)S(1)} %copy.41), channel_id=1, source_target_pairs={{0,1},{1,2},{2,3},{3,4},{4,5},{5,6},{6,7},{7,8},{8,9},{9,10},{10,1... | collective-permute-start | bytes 983048 | tf_op jit(solution)/shard_map/ppermute | solution.py:16
  18.6 13.1 %collective-permute-start.3 = (bf16[1,10,2,32,256]{4,3,2,1,0:T(8,128)(2,1)S(1)}, bf16[1,10,2,32,256]{4,3,2,1,0:T(8,128)(2,1)S(1)}, u32[]{:S(2)}, u32[]{:S(2)}) collective-permute-start(bf16[1,10,2,32,256]{4,3,2,1,0:T(8,128)(2,1)S(1)} %copy.41), channel_id=1, source_target_pairs={{1,0},{2,1},{3,2},{4,3},{5,4},{6,5},{7,6},{8,7},{9,8},{10,9},{11,1... | collective-permute-start | bytes 983048 | tf_op jit(solution)/shard_map/ppermute | solution.py:17
  20.6 5.6 %collective-permute-start = (bf16[1,10,2,32,1]{3,2,1,4,0:T(2,128)(2,1)S(1)}, bf16[1,10,2,32,1]{3,2,1,4,0:T(2,128)(2,1)S(1)}, u32[]{:S(2)}, u32[]{:S(2)}) collective-permute-start(bf16[1,10,2,32,1]{3,2,1,4,0:T(2,128)(2,1)S(1)} %get-tuple-element.19), channel_id=1, source_target_pairs={{0,1},{1,2},{2,3},{3,4},{4,5},{5,6},{6,7},{7,8},{8,9},{9,10},{10,1... | collective-permute-start | bytes 3848 | tf_op jit(solution)/shard_map/ppermute | solution.py:16
  24.2 5.2 %collective-permute-start.1 = (bf16[1,10,2,32,1]{3,2,1,4,0:T(2,128)(2,1)S(1)}, bf16[1,10,2,32,1]{3,2,1,4,0:T(2,128)(2,1)S(1)}, u32[]{:S(2)}, u32[]{:S(2)}) collective-permute-start(bf16[1,10,2,32,1]{3,2,1,4,0:T(2,128)(2,1)S(1)} %get-tuple-element.19), channel_id=1, source_target_pairs={{1,0},{2,1},{3,2},{4,3},{5,4},{6,5},{7,6},{8,7},{9,8},{10,9},{11,1... | collective-permute-start | bytes 3848 | tf_op jit(solution)/shard_map/ppermute | solution.py:17
  26.2 8.1 %copy-start.14 = (bf16[1,10,2,32,1]{3,2,1,4,0:T(2,128)(2,1)}, bf16[1,10,2,32,1]{3,2,1,4,0:T(2,128)(2,1)S(1)}, u32[]{:S(2)}) copy-start(bf16[1,10,2,32,1]{3,2,1,4,0:T(2,128)(2,1)S(1)} %collective-permute-done) | copy-start | bytes 3844
  29.4 4.9 %copy-start.16 = (bf16[1,10,2,32,1]{3,2,1,4,0:T(2,128)(2,1)}, bf16[1,10,2,32,1]{3,2,1,4,0:T(2,128)(2,1)S(1)}, u32[]{:S(2)}) copy-start(bf16[1,10,2,32,1]{3,2,1,4,0:T(2,128)(2,1)S(1)} %collective-permute-done.1) | copy-start | bytes 3844
  34.3 31.9 %all-to-all-start.1 = ((bf16[16,8,27,128]{3,1,2,0:T(8,128)(2,1)}), bf16[16,8,27,128]{3,1,2,0:T(8,128)(2,1)}, u32[]{:S(2)}, u32[]{:S(2)}) async-start(bf16[16,8,27,128]{3,1,2,0:T(8,128)(2,1)} %broadcast_in_dim.8), calls=%async_computation.1 | async-start | bytes 1769472 | tf_op jit(solution)/shard_map/all_to_all | solution.py:44
  50.4 1.1 copy-start.19
  51.5 3.3 %copy-start.2 = (bf16[16,8,27,128]{3,1,0,2:T(8,128)(2,1)}, bf16[16,8,27,128]{3,1,0,2:T(8,128)(2,1)S(1)}, u32[]{:S(2)}) copy-start(bf16[16,8,27,128]{3,1,0,2:T(8,128)(2,1)S(1)} %copy.48) | copy-start | bytes 2654212
  66.2 1.5 copy-start.7
  67.7 3.2 %copy-start.4 = (bf16[16,8,27,128]{3,1,0,2:T(8,128)(2,1)}, bf16[16,8,27,128]{3,1,0,2:T(8,128)(2,1)S(1)}, u32[]{:S(2)}) copy-start(bf16[16,8,27,128]{3,1,0,2:T(8,128)(2,1)S(1)} %copy.52) | copy-start | bytes 2654212
  67.7 3.5 %copy-start.6 = (f32[10,4,32]{1,2,0:T(8,128)S(1)}, f32[10,4,32]{1,2,0:T(8,128)}, u32[]{:S(2)}) copy-start(f32[10,4,32]{1,2,0:T(8,128)} %copy.38) | copy-start | bytes 15364
  70.9 1.1 copy-start
  70.9 1.4 copy-start.1
  71.2 1.7 copy-start.9
  79.9 46.6 %all-to-all-start.3 = ((f32[16,8,27,128]{3,1,2,0:T(8,128)}), f32[16,8,27,128]{3,1,2,0:T(8,128)}, u32[]{:S(2)}, u32[]{:S(2)}) async-start(f32[16,8,27,128]{3,1,2,0:T(8,128)} %copy.67), calls=%async_computation.3 | async-start | bytes 3538944 | tf_op jit(solution)/shard_map/all_to_all | solution.py:54
  126.5 46.8 %all-to-all-start.2 = ((f32[16,8,27,128]{3,1,2,0:T(8,128)}), f32[16,8,27,128]{3,1,2,0:T(8,128)S(1)}, u32[]{:S(2)}, u32[]{:S(2)}) async-start(f32[16,8,27,128]{3,1,2,0:T(8,128)} %copy.65), calls=%async_computation.2 | async-start | bytes 3538944 | tf_op jit(solution)/shard_map/all_to_all | solution.py:54
  132.4 45.5 %copy-start.13 = (bf16[1,10,2,32,1]{3,2,1,4,0:T(2,128)(2,1)S(1)}, bf16[1,10,2,32,1]{3,2,1,4,0:T(2,128)(2,1)}, u32[]{:S(2)}) copy-start(bf16[1,10,2,32,1]{3,2,1,4,0:T(2,128)(2,1)} %copy-done.12) | copy-start | bytes 3844
  132.4 45.5 %copy-start.15 = (bf16[1,10,2,32,1]{3,2,1,4,0:T(2,128)(2,1)S(1)}, bf16[1,10,2,32,1]{3,2,1,4,0:T(2,128)(2,1)}, u32[]{:S(2)}) copy-start(bf16[1,10,2,32,1]{3,2,1,4,0:T(2,128)(2,1)} %copy-done.14) | copy-start | bytes 3844
  132.5 45.5 %copy-start.17 = (bf16[1,10,2,32,1]{3,2,1,4,0:T(2,128)(2,1)S(1)}, bf16[1,10,2,32,1]{3,2,1,4,0:T(2,128)(2,1)}, u32[]{:S(2)}) copy-start(bf16[1,10,2,32,1]{3,2,1,4,0:T(2,128)(2,1)} %copy-done.16) | copy-start | bytes 3844
  134.0 44.4 %collective-permute-start.9 = (f32[8,27,128]{2,0,1:T(8,128)S(1)}, f32[8,27,128]{2,0,1:T(8,128)S(1)}, u32[]{:S(2)}, u32[]{:S(2)}) collective-permute-start(f32[8,27,128]{2,0,1:T(8,128)S(1)} %reduce_sum.19), channel_id=1, source_target_pairs={{0,1},{1,0},{2,3},{3,2},{4,5},{5,4},{6,7},{7,6},{8,9},{9,8},{10,11... | collective-permute-start | bytes 331784 | tf_op jit(solution)/shard_map/ppermute | solution.py:58
  173.4 11.0 %copy-start.5 = (bf16[16,8,27,128]{3,1,0,2:T(8,128)(2,1)S(1)}, bf16[16,8,27,128]{3,1,0,2:T(8,128)(2,1)}, u32[]{:S(2)}) copy-start(bf16[16,8,27,128]{3,1,0,2:T(8,128)(2,1)} %copy-done.4) | copy-start | bytes 2654212
  173.4 11.0 %copy-start.20 = (pred[8,5]{0,1:T(8,128)(4,1)S(1)}, pred[8,5]{0,1:T(8,128)(4,1)}, u32[]{:S(2)}) copy-start(pred[8,5]{0,1:T(8,128)(4,1)} %constant.27) | copy-start | bytes 124
  173.4 9.0 %collective-permute-start.4 = (f32[8,27,128]{2,0,1:T(8,128)S(1)}, f32[8,27,128]{2,0,1:T(8,128)S(1)}, u32[]{:S(2)}, u32[]{:S(2)}) collective-permute-start(f32[8,27,128]{2,0,1:T(8,128)S(1)} %reduce_sum.18), channel_id=1, source_target_pairs={{0,1},{1,0},{2,3},{3,2},{4,5},{5,4},{6,7},{7,6},{8,9},{9,8},{10,11... | collective-permute-start | bytes 331784 | tf_op jit(solution)/shard_map/ppermute | solution.py:58
  178.5 7.9 %collective-permute-start.10 = (f32[8,27,128]{2,0,1:T(8,128)S(1)}, f32[8,27,128]{2,0,1:T(8,128)S(1)}, u32[]{:S(2)}, u32[]{:S(2)}) collective-permute-start(f32[8,27,128]{2,0,1:T(8,128)S(1)} %add.43), channel_id=1, source_target_pairs={{0,2},{1,3},{2,0},{3,1},{4,6},{5,7},{6,4},{7,5},{8,10},{9,11},{10,... | collective-permute-start | bytes 331784 | tf_op jit(solution)/shard_map/ppermute | solution.py:58
  182.5 10.5 %collective-permute-start.5 = (f32[8,27,128]{2,0,1:T(8,128)S(1)}, f32[8,27,128]{2,0,1:T(8,128)S(1)}, u32[]{:S(2)}, u32[]{:S(2)}) collective-permute-start(f32[8,27,128]{2,0,1:T(8,128)S(1)} %add.38), channel_id=1, source_target_pairs={{0,2},{1,3},{2,0},{3,1},{4,6},{5,7},{6,4},{7,5},{8,10},{9,11},{10,... | collective-permute-start | bytes 331784 | tf_op jit(solution)/shard_map/ppermute | solution.py:58
  186.0 9.6 %copy-start.3 = (bf16[16,8,27,128]{3,1,0,2:T(8,128)(2,1)S(1)}, bf16[16,8,27,128]{3,1,0,2:T(8,128)(2,1)}, u32[]{:S(2)}) copy-start(bf16[16,8,27,128]{3,1,0,2:T(8,128)(2,1)} %copy-done.2) | copy-start | bytes 2654212
  186.4 12.2 %collective-permute-start.11 = (f32[8,27,128]{2,0,1:T(8,128)S(1)}, f32[8,27,128]{2,0,1:T(8,128)S(1)}, u32[]{:S(2)}, u32[]{:S(2)}) collective-permute-start(f32[8,27,128]{2,0,1:T(8,128)S(1)} %add.44), channel_id=1, source_target_pairs={{0,4},{1,5},{2,6},{3,7},{4,0},{5,1},{6,2},{7,3},{8,12},{9,13},{10,... | collective-permute-start | bytes 331784 | tf_op jit(solution)/shard_map/ppermute | solution.py:58
  193.0 11.2 %collective-permute-start.6 = (f32[8,27,128]{2,0,1:T(8,128)S(1)}, f32[8,27,128]{2,0,1:T(8,128)S(1)}, u32[]{:S(2)}, u32[]{:S(2)}) collective-permute-start(f32[8,27,128]{2,0,1:T(8,128)S(1)} %add.39), channel_id=1, source_target_pairs={{0,4},{1,5},{2,6},{3,7},{4,0},{5,1},{6,2},{7,3},{8,12},{9,13},{10,... | collective-permute-start | bytes 331784 | tf_op jit(solution)/shard_map/ppermute | solution.py:58
  198.5 11.2 %collective-permute-start.12 = (f32[8,27,128]{2,0,1:T(8,128)S(1)}, f32[8,27,128]{2,0,1:T(8,128)S(1)}, u32[]{:S(2)}, u32[]{:S(2)}) collective-permute-start(f32[8,27,128]{2,0,1:T(8,128)S(1)} %add.45), channel_id=1, source_target_pairs={{0,8},{1,9},{2,10},{3,11},{4,12},{5,13},{6,14},{7,15},{8,0},{9,1},... | collective-permute-start | bytes 331784 | tf_op jit(solution)/shard_map/ppermute | solution.py:58
  204.3 12.2 %collective-permute-start.7 = (f32[8,27,128]{2,0,1:T(8,128)S(1)}, f32[8,27,128]{2,0,1:T(8,128)S(1)}, u32[]{:S(2)}, u32[]{:S(2)}) collective-permute-start(f32[8,27,128]{2,0,1:T(8,128)S(1)} %add.40), channel_id=1, source_target_pairs={{0,8},{1,9},{2,10},{3,11},{4,12},{5,13},{6,14},{7,15},{8,0},{9,1},... | collective-permute-start | bytes 331784 | tf_op jit(solution)/shard_map/ppermute | solution.py:58
  209.8 12.6 %collective-permute-start.13 = (f32[8,27,128]{2,0,1:T(8,128)S(1)}, f32[8,27,128]{2,0,1:T(8,128)S(1)}, u32[]{:S(2)}, u32[]{:S(2)}) collective-permute-start(f32[8,27,128]{2,0,1:T(8,128)S(1)} %add.46), channel_id=1, source_target_pairs={{0,16},{1,17},{2,18},{3,19},{4,20},{5,21},{6,22},{7,23},{8,24},{9,... | collective-permute-start | bytes 331784 | tf_op jit(solution)/shard_map/ppermute | solution.py:58
  216.5 7.0 %collective-permute-start.8 = (f32[8,27,128]{2,0,1:T(8,128)S(1)}, f32[8,27,128]{2,0,1:T(8,128)S(1)}, u32[]{:S(2)}, u32[]{:S(2)}) collective-permute-start(f32[8,27,128]{2,0,1:T(8,128)S(1)} %add.41), channel_id=1, source_target_pairs={{0,16},{1,17},{2,18},{3,19},{4,20},{5,21},{6,22},{7,23},{8,24},{9,... | collective-permute-start | bytes 331784 | tf_op jit(solution)/shard_map/ppermute | solution.py:58

commit v2 on v1

--- a/solution.py
+++ b/solution.py
@@ -48,16 +48,16 @@
     return forward, backward
 
 
-def reduce_grad(grad_full):
+def reduce_grads(grads):
     count = lax.axis_size("dp")
-    parts = grad_full.reshape((count, -1) + grad_full.shape[1:])
-    owned = lax.all_to_all(parts, "dp", 0, 0).sum(axis=0)
     size = lax.axis_size("space")
-    step = 1
-    while step < size:
-        owned = owned + lax.ppermute(owned, "space", [(i, i ^ step) for i in range(size)])
-        step *= 2
-    return owned
+    parts = jnp.stack([g.reshape((count, -1) + g.shape[1:]) for g in grads], axis=1)
+    owned = lax.all_to_all(parts.astype(jnp.bfloat16), "dp", 0, 0)
+    owned = owned.astype(jnp.float32).sum(axis=0)
+    pieces = lax.all_to_all(owned.reshape(size, -1), "space", 0, 0).sum(axis=0)
+    copies = jnp.broadcast_to(pieces[None], (size,) + pieces.shape)
+    full = lax.all_to_all(copies, "space", 0, 0).reshape(owned.shape)
+    return [full[i] for i in range(len(grads))]
 
 
 def on_device(inputs, land_mask, weight_one, weight_two, cotangent):
@@ -82,12 +82,13 @@
     prediction = (mask_own * conv(act_pad, k2)).astype(jnp.bfloat16)
 
     back_own = back_two_wide[:, :, HALO : HALO + rows]
-    grad_two = reduce_grad(weight_grad(act_pad, back_own))
+    grad_two_terms = weight_grad(act_pad, back_own)
 
     pull_one = conv(pad_depth_cols(back_two_wide), k2_t)
     back_one = (pull_one * mask_mid * sigma * (1.0 + pre_one * (1.0 - sigma))).astype(jnp.bfloat16)
     in_mid = pad_depth_cols(in_wide[:, :, 1 : rows + 3])
-    grad_one = reduce_grad(weight_grad(in_mid, back_one[:, :, 1 : rows + 1]))
+    grad_one_terms = weight_grad(in_mid, back_one[:, :, 1 : rows + 1])
+    grad_one, grad_two = reduce_grads([grad_one_terms, grad_two_terms])
     input_grad = conv(pad_depth_cols(back_one), k1_t).astype(jnp.bfloat16)
     return (prediction, input_grad, grad_one, grad_two)
 

time: 227 us -> 181 us (0.80)
  starting transfers between devices: 80.9 us -> 52.7 us
  waiting for transfers between devices: 88.6 us -> 69.5 us
  local copies, waits for them, and re-layouts: 22.3 us -> 27.3 us
  other arithmetic: 10.9 us -> 8.28 us
    ppermute x10 -> x0, starting transfers between devices: 41.6 us -> none  [reduce_grad(): lax.ppermute(owned, 'space', [(i, i ^ step) for i in range(size)])]
    all_to_all x2 -> x3, waiting for transfers between devices: 72.4 us -> 57.3 us  [the longest x1 39.1 us: reduce_grads(): owned = lax.all_to_all(parts.astype(jnp.bfloat16), 'dp', 0, 0)]
    all_to_all x2 -> x3, starting transfers between devices: 10.3 us -> 23.8 us  [the longest x1 14.3 us: reduce_grads(): pieces = lax.all_to_all(owned.reshape(size, -1), 'space', 0, 0).sum(axis=0)]
    ppermute x10 -> x0, waiting for transfers between devices: 3.86 us -> none  [reduce_grad(): lax.ppermute(owned, 'space', [(i, i ^ step) for i in range(size)])]
    unnamed x46 -> x54, local copies, waits for them, and re-layouts: 4.47 us -> 6.61 us
  transfers between devices with their start and end apart: 18 -> 9, of which waited for: 7 -> 5; matrix products, arithmetic and copies ran while one was open for 16% -> 16% of each run, Pallas kernels for 0% -> 0%
where the time goes in v2:
time: 181 us; the launch traced here: 180 us
  waiting for transfers between devices  69.5 us (38%)
  starting transfers between devices  52.7 us (29%)
  local copies, waits for them, and re-layouts  27.3 us (15%)
  matrix products  20.9 us (12%)
  other arithmetic  8.28 us (5%)
    all_to_all x1, waiting for transfers between devices, reduce_grads(): owned = lax.all_to_all(parts.astype(jnp.bfloat16), 'dp', 0, 0)  39.1 us
    all_to_all x2, starting transfers between devices, gather_kernel(): full = lax.all_to_all(copies, 'dp', 0, 0).reshape((-1,) + local.shape[1:])  16.6 us
    all_to_all x1, starting transfers between devices, reduce_grads(): pieces = lax.all_to_all(owned.reshape(size, -1), 'space', 0, 0).sum(axis=0)  14.3 us
    conv_general_dilated x4, matrix products, conv(): lax.conv_general_dilated(padded, kernel, (1, 1, 1), 'VALID', dimension_nu...  10.6 us
    conv_general_dilated x2, matrix products, weight_grad(): lax.conv_general_dilated(padded, back, (1, 1, 1), 'VALID', dimension_numb...  10.3 us
    all_to_all x1, waiting for transfers between devices, reduce_grads(): full = lax.all_to_all(copies, 'space', 0, 0).reshape(owned.shape)  9.53 us
    all_to_all x2, waiting for transfers between devices, gather_kernel(): full = lax.all_to_all(copies, 'dp', 0, 0).reshape((-1,) + local.shape[1:])  8.91 us
    all_to_all x1, waiting for transfers between devices, reduce_grads(): pieces = lax.all_to_all(owned.reshape(size, -1), 'space', 0, 0).sum(axis=0)  8.7 us
  transfers between devices with their start and end apart: 9, of which 5 were waited for; matrix products, arithmetic and copies ran while one was open for 16% of the time, Pallas kernels for 0%

profile of v2, /device:TPU:1, one launch (start us, length us, event | category | flops | bytes accessed | tf_op | source)
XLA Modules:
  0.0 180.0 jit_solution(5364694748325586924)
XLA Ops:
  0.7 0.9 convert_element_type.66
  1.6 1.1 broadcast_in_dim.9
  2.7 8.7 %all-to-all-start = ((bf16[16,8,27,128]{3,1,2,0:T(8,128)(2,1)}), bf16[16,8,27,128]{3,1,2,0:T(8,128)(2,1)S(1)}, u32[]{:S(2)}, u32[]{:S(2)}) async-start(bf16[16,8,27,128]{3,1,2,0:T(8,128)(2,1)} %broadcast_in_dim.9), calls=%async_computation | async-start | bytes 1769472 | tf_op jit(solution)/shard_map/all_to_all | solution.py:44
  11.4 0.3 copy.42
  11.8 0.8 fusion.38
  12.6 1.1 pad_maximum_fusion.2
  13.8 4.8 %collective-permute-start.2 = (bf16[1,10,2,32,256]{4,3,2,1,0:T(8,128)(2,1)S(1)}, bf16[1,10,2,32,256]{4,3,2,1,0:T(8,128)(2,1)S(1)}, u32[]{:S(2)}, u32[]{:S(2)}) collective-permute-start(bf16[1,10,2,32,256]{4,3,2,1,0:T(8,128)(2,1)S(1)} %copy.43), channel_id=1, source_target_pairs={{0,1},{1,2},{2,3},{3,4},{4,5},{5,6},{6,7},{7,8},{8,9},{9,10},{10,1... | collective-permute-start | bytes 983048 | tf_op jit(solution)/shard_map/ppermute | solution.py:16
  18.7 1.9 %collective-permute-start.3 = (bf16[1,10,2,32,256]{4,3,2,1,0:T(8,128)(2,1)S(1)}, bf16[1,10,2,32,256]{4,3,2,1,0:T(8,128)(2,1)S(1)}, u32[]{:S(2)}, u32[]{:S(2)}) collective-permute-start(bf16[1,10,2,32,256]{4,3,2,1,0:T(8,128)(2,1)S(1)} %copy.43), channel_id=1, source_target_pairs={{1,0},{2,1},{3,2},{4,3},{5,4},{6,5},{7,6},{8,7},{9,8},{10,9},{11,1... | collective-permute-start | bytes 983048 | tf_op jit(solution)/shard_map/ppermute | solution.py:17
  20.6 3.6 %collective-permute-start = (bf16[1,10,2,32,1]{3,2,1,4,0:T(2,128)(2,1)S(1)}, bf16[1,10,2,32,1]{3,2,1,4,0:T(2,128)(2,1)S(1)}, u32[]{:S(2)}, u32[]{:S(2)}) collective-permute-start(bf16[1,10,2,32,1]{3,2,1,4,0:T(2,128)(2,1)S(1)} %get-tuple-element.21), channel_id=1, source_target_pairs={{0,1},{1,2},{2,3},{3,4},{4,5},{5,6},{6,7},{7,8},{8,9},{9,10},{10,1... | collective-permute-start | bytes 3848 | tf_op jit(solution)/shard_map/ppermute | solution.py:16
  24.3 1.9 %collective-permute-start.1 = (bf16[1,10,2,32,1]{3,2,1,4,0:T(2,128)(2,1)S(1)}, bf16[1,10,2,32,1]{3,2,1,4,0:T(2,128)(2,1)S(1)}, u32[]{:S(2)}, u32[]{:S(2)}) collective-permute-start(bf16[1,10,2,32,1]{3,2,1,4,0:T(2,128)(2,1)S(1)} %get-tuple-element.21), channel_id=1, source_target_pairs={{1,0},{2,1},{3,2},{4,3},{5,4},{6,5},{7,6},{8,7},{9,8},{10,9},{11,1... | collective-permute-start | bytes 3848 | tf_op jit(solution)/shard_map/ppermute | solution.py:17
  26.3 3.3 %collective-permute-done.1 = bf16[1,10,2,32,1]{3,2,1,4,0:T(2,128)(2,1)S(1)} collective-permute-done((bf16[1,10,2,32,1]{3,2,1,4,0:T(2,128)(2,1)S(1)}, bf16[1,10,2,32,1]{3,2,1,4,0:T(2,128)(2,1)S(1)}, u32[]{:S(2)}, u32[]{:S(2)}) %collective-permute-start.1) | collective-permute-done | bytes 1312 | tf_op jit(solution)/shard_map/ppermute | solution.py:17
  29.5 0.8 copy.40
  30.4 1.5 copy.45
  31.8 1.5 copy.46
  33.3 1.1 broadcast_in_dim.10
  34.4 7.9 %all-to-all-start.1 = ((bf16[16,8,27,128]{3,1,2,0:T(8,128)(2,1)}), bf16[16,8,27,128]{3,1,2,0:T(8,128)(2,1)}, u32[]{:S(2)}, u32[]{:S(2)}) async-start(bf16[16,8,27,128]{3,1,2,0:T(8,128)(2,1)} %broadcast_in_dim.10), calls=%async_computation.1 | async-start | bytes 1769472 | tf_op jit(solution)/shard_map/all_to_all | solution.py:44
  42.3 3.8 %pad_maximum_fusion = bf16[1,10,6,32,256]{4,0,3,2,1:T(2,128)(2,1)S(1)} fusion(bf16[1,10,2,32,256]{4,0,3,2,1:T(2,128)(2,1)} %copy.46, bf16[1,10,2,32,128]{4,0,3,2,1:T(2,128)(2,1)S(1)} %fusion.38, bf16[1,10,2,32,128]{4,0,3,2,1:T(2,128)(2,1)S(1)} %copy.42, bf16[1,10,2,32,256]{4,0,3,2,1:T(2,128)(2,1)} %copy.45), kind=kLoop, calls=%fused_computation.1 | loop fusion | flops 3932160 | bytes 1966080 | tf_op jit(solution)/shard_map/concatenate | solution.py:18
  46.1 2.3 %fusion.56 = (bf16[1,10,6,32,128]{4,0,3,2,1:T(2,128)(2,1)S(1)}, bf16[1,10,6,32,128]{4,0,3,2,1:T(2,128)(2,1)S(1)}) fusion(bf16[1,10,6,32,256]{4,0,3,2,1:T(2,128)(2,1)S(1)} %pad_maximum_fusion), kind=kLoop, calls=%fused_computation.82 | loop fusion | bytes 1966080 | tf_op jit(solution)/shard_map/slice | solution.py:71
  48.4 1.6 copy_bitcast_fusion
  49.9 0.2 pad.7.clone
  50.2 0.2 pad.11.clone
  50.5 0.8 slice.56
  51.3 0.2 copy.50
  51.5 3.3 %add_divide_fusion = (f32[10,4,8,5,128]{4,2,3,1,0:T(8,128)S(1)}, f32[10,4,8,5,128]{4,2,3,1,0:T(8,128)S(1)}, f32[10,4,8,5,128]{4,2,3,1,0:T(8,128)S(1)}) fusion(bf16[128,3,3,3,128]{4,0,3,2,1:T(8,128)(2,1)S(1)} %bitcast.68, bf16[10,6,1,7,2,128]{5,3,4,1,0,2:T(8,128)(2,1)S(1)} %slice.51, bf16[10,6,1,8,5,128]{5,3,4,1,0,2:T(8,128)(2,1)S(1)} %copy.49, ...), kind=kOutput, calls=%fused_computation.27 | convolution fusion | flops 1325424640 | bytes 4171816 | tf_op jit(solution)/shard_map/conv_general_dilated | solution.py:26
  54.9 0.2 copy.60
  55.1 1.1 copy.61
  56.2 1.1 copy.51
  57.3 8.9 %all-to-all-done.1 = bf16[16,8,27,128]{3,1,2,0:T(8,128)(2,1)} async-done(((bf16[16,8,27,128]{3,1,2,0:T(8,128)(2,1)}), bf16[16,8,27,128]{3,1,2,0:T(8,128)(2,1)}, u32[]{:S(2)}, u32[]{:S(2)}) %all-to-all-start.1) | async-done | bytes 884768 | tf_op jit(solution)/shard_map/all_to_all | solution.py:44
  66.2 1.4 copy.54
  67.7 3.2 %convolution_select_fusion = f32[10,4,8,5,128]{4,2,3,1,0:T(8,128)S(1)} fusion(bf16[128,3,3,3,128]{4,0,3,2,1:T(8,128)(2,1)S(1)} %bitcast.66, bf16[10,6,1,7,2,128]{5,3,4,1,0,2:T(8,128)(2,1)S(1)} %copy-done.10, bf16[10,6,1,8,5,128]{5,3,4,1,0,2:T(8,128)(2,1)S(1)} %copy.58, pred[8,5]{0,1:T(8,128)(4,1)S(1)} %copy-done.22), kind=kOutput, calls=%fused_computation.8 | convolution fusion | flops 1323991040 | bytes 2533416 | tf_op jit(solution)/shard_map/conv_general_dilated | solution.py:26
  70.9 0.2 copy.59
  71.2 0.9 copy-done
  72.1 0.2 copy-done.1
  72.3 0.5 fusion.17
  72.8 0.7 copy-done.2
  73.5 0.2 slice.63
  73.7 5.1 %convolution_convert_fusion.1 = bf16[128,3,3,3,128]{4,0,3,2,1:T(8,128)(2,1)S(1)} fusion(bf16[1,10,6,32,256]{4,0,3,2,1:T(2,128)(2,1)S(1)} %pad_maximum_fusion, bf16[1,10,2,32,128]{4,2,3,1,0:T(2,128)(2,1)S(1)} %slice.63), kind=kOutput, calls=%fused_computation.7 | convolution fusion | flops 517914624 | bytes 1703936 | tf_op jit(solution)/shard_map/conv_general_dilated | solution.py:33
  78.8 5.2 %convolution_convert_fusion = bf16[128,3,3,3,128]{4,0,3,2,1:T(8,128)(2,1)S(1)} fusion(bf16[1,10,4,32,128]{4,2,3,1,0:T(4,128)(2,1)S(1)} %bitcast.63, bf16[1,10,2,32,128]{4,3,2,1,0:T(8,128)(2,1)S(1)} %copy-done.12, f32[10,2,32]{2,1,0:T(2,128)S(1)} %get-tuple-element.22), kind=kOutput, calls=%fused_computation.6 | convolution fusion | flops 518160384 | bytes 1378816 | tf_op jit(solution)/shard_map/conv_general_dilated | solution.py:33
  84.1 0.2 pad_maximum_fusion.1
  84.2 1.5 copy.79
  85.8 4.1 %all-to-all-start.2 = ((bf16[16,2,8,27,128]{4,2,3,1,0:T(8,128)(2,1)}), bf16[16,2,8,27,128]{4,2,3,1,0:T(8,128)(2,1)S(1)}, u32[]{:S(2)}, u32[]{:S(2)}) async-start(bf16[16,2,8,27,128]{4,2,3,1,0:T(8,128)(2,1)} %copy.79), calls=%async_computation.2 | async-start | bytes 3538944 | tf_op jit(solution)/shard_map/all_to_all | solution.py:55
  90.0 0.8 copy.39
  90.8 0.1 pad.13
  90.9 0.1 pad.9
  91.2 0.7 slice.60
  91.9 39.1 %all-to-all-done.2 = bf16[16,2,8,27,128]{4,2,3,1,0:T(8,128)(2,1)S(1)} async-done(((bf16[16,2,8,27,128]{4,2,3,1,0:T(8,128)(2,1)}), bf16[16,2,8,27,128]{4,2,3,1,0:T(8,128)(2,1)S(1)}, u32[]{:S(2)}, u32[]{:S(2)}) %all-to-all-start.2) | async-done | bytes 1769504 | tf_op jit(solution)/shard_map/all_to_all | solution.py:55
  130.9 0.2 convert_reduce_fusion
  131.2 1.0 all_to_all.25
  132.2 14.3 %all-to-all-start.3 = ((f32[32,1,1728]{2,1,0:T(1,128)}), f32[32,1,1728]{2,1,0:T(1,128)S(1)}, u32[]{:S(2)}, u32[]{:S(2)}) async-start(f32[32,1,1728]{2,1,0:T(1,128)} %all_to_all.25), calls=%async_computation.3 | async-start | bytes 458752 | tf_op jit(solution)/shard_map/all_to_all | solution.py:57
  146.5 2.5 %fusion.2 = bf16[10,2,8,5,128]{4,2,3,1,0:T(8,128)(2,1)S(1)} fusion(bf16[128,3,3,3,128]{4,0,3,2,1:T(8,128)(2,1)S(1)} %bitcast.69, bf16[10,4,1,7,2,128]{5,3,4,1,0,2:T(8,128)(2,1)} %slice.60, bf16[10,4,1,8,5,128]{5,3,4,1,0,2:T(8,128)(2,1)S(1)} %copy.63, pred[8,5]{0,1:T(8,128)(4,1)S(1)} %copy-done.23), kind=kOutput, calls=%fused_computation.12 | convolution fusion | flops 662528000 | bytes 1642536 | tf_op jit(solution)/shard_map/conv_general_dilated | solution.py:26
  149.1 0.2 copy.64
  149.4 0.7 copy.74
  150.2 8.7 %all-to-all-done.3 = f32[32,1,1728]{2,1,0:T(1,128)S(1)} async-done(((f32[32,1,1728]{2,1,0:T(1,128)}), f32[32,1,1728]{2,1,0:T(1,128)S(1)}, u32[]{:S(2)}, u32[]{:S(2)}) %all-to-all-start.3) | async-done | bytes 221216 | tf_op jit(solution)/shard_map/all_to_all | solution.py:57
  158.9 0.1 reduce_sum.19
  159.0 0.8 broadcast_in_dim.11
  159.8 5.4 %all-to-all-start.4 = ((f32[32,1,1728]{2,1,0:T(1,128)}), f32[32,1,1728]{2,1,0:T(1,128)S(1)}, u32[]{:S(2)}, u32[]{:S(2)}) async-start(f32[32,1,1728]{2,1,0:T(1,128)} %broadcast_in_dim.11), calls=%async_computation.4 | async-start | bytes 458752 | tf_op jit(solution)/shard_map/all_to_all | solution.py:59
  165.3 1.6 convolution_select_fusion.3
  166.9 0.2 copy.55
  167.1 0.4 fusion.41
  167.5 0.7 copy.73
  168.2 9.5 %all-to-all-done.4 = f32[32,1,1728]{2,1,0:T(1,128)S(1)} async-done(((f32[32,1,1728]{2,1,0:T(1,128)}), f32[32,1,1728]{2,1,0:T(1,128)S(1)}, u32[]{:S(2)}, u32[]{:S(2)}) %all-to-all-start.4) | async-done | bytes 221216 | tf_op jit(solution)/shard_map/all_to_all | solution.py:59
  177.7 0.6 slice_reduce_fusion
  178.5 0.7 copy.75
  179.3 0.7 copy.76
  (64 shorter events, 1.0 us)
Async XLA Ops:
  0.6 10.8 %copy-start.13 = (bf16[1,10,2,32,128]{4,3,2,1,0:T(8,128)(2,1)S(1)}, bf16[1,10,2,32,128]{4,3,2,1,0:T(8,128)(2,1)}, u32[]{:S(2)}) copy-start(bf16[1,10,2,32,128]{4,3,2,1,0:T(8,128)(2,1)} %param.5) | copy-start | bytes 491524
  0.6 11.1 %copy-start.21 = (s32[1,10,2,32]{3,2,1,0:T(2,128)S(1)}, s32[1,10,2,32]{3,2,1,0:T(2,128)}, u32[]{:S(2)}) copy-start(s32[1,10,2,32]{3,2,1,0:T(2,128)} %param.6) | copy-start | bytes 7684
  0.7 11.1 %copy-start.11 = (bf16[1,10,2,32,128]{4,3,2,1,0:T(8,128)(2,1)S(1)}, bf16[1,10,2,32,128]{4,3,2,1,0:T(8,128)(2,1)}, u32[]{:S(2)}) copy-start(bf16[1,10,2,32,128]{4,3,2,1,0:T(8,128)(2,1)} %param.9) | copy-start | bytes 491524
  2.7 30.6 %all-to-all-start = ((bf16[16,8,27,128]{3,1,2,0:T(8,128)(2,1)}), bf16[16,8,27,128]{3,1,2,0:T(8,128)(2,1)S(1)}, u32[]{:S(2)}, u32[]{:S(2)}) async-start(bf16[16,8,27,128]{3,1,2,0:T(8,128)(2,1)} %broadcast_in_dim.9), calls=%async_computation | async-start | bytes 1769472 | tf_op jit(solution)/shard_map/all_to_all | solution.py:44
  11.4 14.8 %copy-start.14 = (f32[8,27,128]{2,0,1:T(8,128)S(1)}, f32[8,27,128]{2,0,1:T(8,128)}, u32[]{:S(2)}) copy-start(f32[8,27,128]{2,0,1:T(8,128)} %param.8) | copy-start | bytes 331780
  11.8 20.1 %copy-start.15 = (bf16[1,10,2,32,1]{3,2,1,4,0:T(2,128)(2,1)}, bf16[1,10,2,32,1]{3,2,1,4,0:T(2,128)(2,1)S(1)}, u32[]{:S(2)}) copy-start(bf16[1,10,2,32,1]{3,2,1,4,0:T(2,128)(2,1)S(1)} %get-tuple-element.21) | copy-start | bytes 3844
  13.8 16.5 %collective-permute-start.2 = (bf16[1,10,2,32,256]{4,3,2,1,0:T(8,128)(2,1)S(1)}, bf16[1,10,2,32,256]{4,3,2,1,0:T(8,128)(2,1)S(1)}, u32[]{:S(2)}, u32[]{:S(2)}) collective-permute-start(bf16[1,10,2,32,256]{4,3,2,1,0:T(8,128)(2,1)S(1)} %copy.43), channel_id=1, source_target_pairs={{0,1},{1,2},{2,3},{3,4},{4,5},{5,6},{6,7},{7,8},{8,9},{9,10},{10,1... | collective-permute-start | bytes 983048 | tf_op jit(solution)/shard_map/ppermute | solution.py:16
  18.7 13.1 %collective-permute-start.3 = (bf16[1,10,2,32,256]{4,3,2,1,0:T(8,128)(2,1)S(1)}, bf16[1,10,2,32,256]{4,3,2,1,0:T(8,128)(2,1)S(1)}, u32[]{:S(2)}, u32[]{:S(2)}) collective-permute-start(bf16[1,10,2,32,256]{4,3,2,1,0:T(8,128)(2,1)S(1)} %copy.43), channel_id=1, source_target_pairs={{1,0},{2,1},{3,2},{4,3},{5,4},{6,5},{7,6},{8,7},{9,8},{10,9},{11,1... | collective-permute-start | bytes 983048 | tf_op jit(solution)/shard_map/ppermute | solution.py:17
  20.6 5.6 %collective-permute-start = (bf16[1,10,2,32,1]{3,2,1,4,0:T(2,128)(2,1)S(1)}, bf16[1,10,2,32,1]{3,2,1,4,0:T(2,128)(2,1)S(1)}, u32[]{:S(2)}, u32[]{:S(2)}) collective-permute-start(bf16[1,10,2,32,1]{3,2,1,4,0:T(2,128)(2,1)S(1)} %get-tuple-element.21), channel_id=1, source_target_pairs={{0,1},{1,2},{2,3},{3,4},{4,5},{5,6},{6,7},{7,8},{8,9},{9,10},{10,1... | collective-permute-start | bytes 3848 | tf_op jit(solution)/shard_map/ppermute | solution.py:16
  24.3 5.2 %collective-permute-start.1 = (bf16[1,10,2,32,1]{3,2,1,4,0:T(2,128)(2,1)S(1)}, bf16[1,10,2,32,1]{3,2,1,4,0:T(2,128)(2,1)S(1)}, u32[]{:S(2)}, u32[]{:S(2)}) collective-permute-start(bf16[1,10,2,32,1]{3,2,1,4,0:T(2,128)(2,1)S(1)} %get-tuple-element.21), channel_id=1, source_target_pairs={{1,0},{2,1},{3,2},{4,3},{5,4},{6,5},{7,6},{8,7},{9,8},{10,9},{11,1... | collective-permute-start | bytes 3848 | tf_op jit(solution)/shard_map/ppermute | solution.py:17
  26.2 8.1 %copy-start.17 = (bf16[1,10,2,32,1]{3,2,1,4,0:T(2,128)(2,1)}, bf16[1,10,2,32,1]{3,2,1,4,0:T(2,128)(2,1)S(1)}, u32[]{:S(2)}) copy-start(bf16[1,10,2,32,1]{3,2,1,4,0:T(2,128)(2,1)S(1)} %collective-permute-done) | copy-start | bytes 3844
  29.5 4.9 %copy-start.19 = (bf16[1,10,2,32,1]{3,2,1,4,0:T(2,128)(2,1)}, bf16[1,10,2,32,1]{3,2,1,4,0:T(2,128)(2,1)S(1)}, u32[]{:S(2)}) copy-start(bf16[1,10,2,32,1]{3,2,1,4,0:T(2,128)(2,1)S(1)} %collective-permute-done.1) | copy-start | bytes 3844
  34.4 31.9 %all-to-all-start.1 = ((bf16[16,8,27,128]{3,1,2,0:T(8,128)(2,1)}), bf16[16,8,27,128]{3,1,2,0:T(8,128)(2,1)}, u32[]{:S(2)}, u32[]{:S(2)}) async-start(bf16[16,8,27,128]{3,1,2,0:T(8,128)(2,1)} %broadcast_in_dim.10), calls=%async_computation.1 | async-start | bytes 1769472 | tf_op jit(solution)/shard_map/all_to_all | solution.py:44
  50.4 1.1 copy-start.22
  51.5 3.3 %copy-start.6 = (bf16[16,8,27,128]{3,1,0,2:T(8,128)(2,1)}, bf16[16,8,27,128]{3,1,0,2:T(8,128)(2,1)S(1)}, u32[]{:S(2)}) copy-start(bf16[16,8,27,128]{3,1,0,2:T(8,128)(2,1)S(1)} %copy.50) | copy-start | bytes 2654212
  66.2 1.5 copy-start.10
  67.7 3.2 %copy-start.4 = (bf16[16,8,27,128]{3,1,0,2:T(8,128)(2,1)}, bf16[16,8,27,128]{3,1,0,2:T(8,128)(2,1)S(1)}, u32[]{:S(2)}) copy-start(bf16[16,8,27,128]{3,1,0,2:T(8,128)(2,1)S(1)} %copy.54) | copy-start | bytes 2654212
  67.7 3.5 %copy-start.9 = (f32[10,4,32]{1,2,0:T(8,128)S(1)}, f32[10,4,32]{1,2,0:T(8,128)}, u32[]{:S(2)}) copy-start(f32[10,4,32]{1,2,0:T(8,128)} %copy.40) | copy-start | bytes 15364
  70.9 1.1 copy-start
  70.9 1.4 copy-start.1
  72.8 0.7 copy-start.2
  73.7 5.1 %copy-start.12 = (bf16[1,10,2,32,128]{4,3,2,1,0:T(8,128)(2,1)S(1)}, bf16[1,10,2,32,128]{4,3,2,1,0:T(8,128)(2,1)}, u32[]{:S(2)}) copy-start(bf16[1,10,2,32,128]{4,3,2,1,0:T(8,128)(2,1)} %param.9) | copy-start | bytes 491524
  85.8 4.2 %copy-start.16 = (bf16[1,10,2,32,1]{3,2,1,4,0:T(2,128)(2,1)S(1)}, bf16[1,10,2,32,1]{3,2,1,4,0:T(2,128)(2,1)}, u32[]{:S(2)}) copy-start(bf16[1,10,2,32,1]{3,2,1,4,0:T(2,128)(2,1)} %copy-done.15) | copy-start | bytes 3844
  85.8 4.2 %copy-start.18 = (bf16[1,10,2,32,1]{3,2,1,4,0:T(2,128)(2,1)S(1)}, bf16[1,10,2,32,1]{3,2,1,4,0:T(2,128)(2,1)}, u32[]{:S(2)}) copy-start(bf16[1,10,2,32,1]{3,2,1,4,0:T(2,128)(2,1)} %copy-done.17) | copy-start | bytes 3844
  85.8 4.2 %copy-start.20 = (bf16[1,10,2,32,1]{3,2,1,4,0:T(2,128)(2,1)S(1)}, bf16[1,10,2,32,1]{3,2,1,4,0:T(2,128)(2,1)}, u32[]{:S(2)}) copy-start(bf16[1,10,2,32,1]{3,2,1,4,0:T(2,128)(2,1)} %copy-done.19) | copy-start | bytes 3844
  85.8 5.0 %copy-start.3 = (bf16[10,4,1,32,128]{4,1,3,0,2:T(4,128)(2,1)S(1)}, bf16[10,4,1,32,128]{4,1,3,0,2:T(4,128)(2,1)}, u32[]{:S(2)}) copy-start(bf16[10,4,1,32,128]{4,1,3,0,2:T(4,128)(2,1)} %copy-done.2) | copy-start | bytes 983044
  85.8 45.2 %all-to-all-start.2 = ((bf16[16,2,8,27,128]{4,2,3,1,0:T(8,128)(2,1)}), bf16[16,2,8,27,128]{4,2,3,1,0:T(8,128)(2,1)S(1)}, u32[]{:S(2)}, u32[]{:S(2)}) async-start(bf16[16,2,8,27,128]{4,2,3,1,0:T(8,128)(2,1)} %copy.79), calls=%async_computation.2 | async-start | bytes 3538944 | tf_op jit(solution)/shard_map/all_to_all | solution.py:55
  91.9 54.6 %copy-start.7 = (bf16[16,8,27,128]{3,1,0,2:T(8,128)(2,1)S(1)}, bf16[16,8,27,128]{3,1,0,2:T(8,128)(2,1)}, u32[]{:S(2)}) copy-start(bf16[16,8,27,128]{3,1,0,2:T(8,128)(2,1)} %copy-done.6) | copy-start | bytes 2654212
  91.9 54.7 %copy-start.23 = (pred[8,5]{0,1:T(8,128)(4,1)S(1)}, pred[8,5]{0,1:T(8,128)(4,1)}, u32[]{:S(2)}) copy-start(pred[8,5]{0,1:T(8,128)(4,1)} %constant.27) | copy-start | bytes 124
  132.2 26.7 %all-to-all-start.3 = ((f32[32,1,1728]{2,1,0:T(1,128)}), f32[32,1,1728]{2,1,0:T(1,128)S(1)}, u32[]{:S(2)}, u32[]{:S(2)}) async-start(f32[32,1,1728]{2,1,0:T(1,128)} %all_to_all.25), calls=%async_computation.3 | async-start | bytes 458752 | tf_op jit(solution)/shard_map/all_to_all | solution.py:57
  149.1 16.2 %copy-start.5 = (bf16[16,8,27,128]{3,1,0,2:T(8,128)(2,1)S(1)}, bf16[16,8,27,128]{3,1,0,2:T(8,128)(2,1)}, u32[]{:S(2)}) copy-start(bf16[16,8,27,128]{3,1,0,2:T(8,128)(2,1)} %copy-done.4) | copy-start | bytes 2654212
  159.8 17.9 %all-to-all-start.4 = ((f32[32,1,1728]{2,1,0:T(1,128)}), f32[32,1,1728]{2,1,0:T(1,128)S(1)}, u32[]{:S(2)}, u32[]{:S(2)}) async-start(f32[32,1,1728]{2,1,0:T(1,128)} %broadcast_in_dim.11), calls=%async_computation.4 | async-start | bytes 458752 | tf_op jit(solution)/shard_map/all_to_all | solution.py:59
  165.2 1.8 %copy-start.8 = (f32[10,2,32]{1,2,0:T(8,128)S(1)}, f32[10,2,32]{1,2,0:T(8,128)}, u32[]{:S(2)}) copy-start(f32[10,2,32]{1,2,0:T(8,128)} %copy.39) | copy-start | bytes 7684
